TPU v7x, 128 devices: a whole 4x4x4 slice. The times are simulated.
128 devices in a mesh: seq: 4 (over x_hi, core), tensor: 32 (over y, x_lo, z).
Axes of the slice: x: 4 (x_hi: 2, x_lo: 2; x = x_hi * 2 + x_lo), y: 4, z: 4, core: 2. Of those that a mesh axis runs over, the one named last changes fastest.
Arguments:
- hidden_in: bfloat16 [8192, 4608], P(('seq', 'tensor'))
- norm_gain: float32 [4608], replicated, may hold values from 0.5 to 1.5
- query_weight: bfloat16 [4608, 4096], P(None, 'tensor')
- key_weight: bfloat16 [4608, 2048], P(None, 'tensor'), may hold values from -0.09375 to 0.09375
- value_weight: bfloat16 [4608, 2048], P(None, 'tensor'), may hold values from -0.09375 to 0.09375
- out_weight: bfloat16 [4096, 4608], P('tensor'), may hold values from -0.09375 to 0.09375
- post_gain: float32 [4608], replicated, may hold values from 0.5 to 1.5
- seg_lengths: int32 [3], replicated, may hold values from 256 to 4096, as said below
- segment_ids: int32 [8192], replicated, may hold values from 0 to 2, as said below
- slot_map: int32 [3], replicated, may hold values from 0 to 2, each once
Outputs:
- hidden_out: bfloat16 [8192, 4608], P(('seq', 'tensor'))
- key_cache: bfloat16 [3, 4096, 2048], P(None, 'seq', 'tensor')
- value_cache: bfloat16 [3, 4096, 2048], P(None, 'seq', 'tensor')
Inputs may be any that keep to these rules, and one draw needn't show every extreme that they name: `seg_lengths`: the 3 lengths sum to 8192; the second request is the longest, with exactly 4096 tokens. `segment_ids`: requests follow one another in order: request r holds seg_lengths[r] consecutive tokens, starting where request r - 1 ends. `slot_map`: each cache slot is named by exactly one request.
All inputs are finite; a program needn't handle non-finite values.
Results may differ from a plain program's by a relative error of at most 0.02.
Values may be sent and summed in bfloat16 or wider, within the bound.
No kernel may reach another device: no remote copies, remote signals or barrier semaphores. Data moves between devices by JAX's collectives and lax.ppermute only.
A program may use at most 128 MiB of HBM per device.

v0:
```python
import jax
import jax.numpy as jnp
import numpy as np
from jax import lax
from jax.sharding import Mesh
from jax.sharding import PartitionSpec as P

HD = 128


EPSILON = 1e-06
SOFTCAP = 50.0
QUERY_SCALE = 144.0 ** (-0.5)
SCORE_SHIFT = 20.0
ROPE_BASE = 10000.0
KEY_TILE = 512
Q_CHUNKS = 2


def rms_scale(values, gain):
    mean_sq = jnp.mean(values * values, axis=-1, keepdims=True)
    return values * lax.rsqrt(mean_sq + EPSILON) * gain


def rotate(values, positions):
    head_dim = values.shape[-1]
    half_dim = head_dim // 2
    freqs = ROPE_BASE ** (-2.0 * jnp.arange(half_dim, dtype=jnp.float32) / head_dim)
    angles = positions.astype(jnp.float32)[:, None] * freqs[None, :]
    cosine = jnp.cos(angles)[:, None, :]
    sine = jnp.sin(angles)[:, None, :]
    first = values[..., :half_dim]
    second = values[..., half_dim:]
    return jnp.concatenate(
        [first * cosine - second * sine, second * cosine + first * sine], axis=-1
    )


def segment_starts_of(row_segments, seg_lengths):
    starts = jnp.cumsum(seg_lengths) - seg_lengths
    request_ids = jnp.arange(seg_lengths.shape[0], dtype=jnp.int32)
    return jnp.sum(
        jnp.where(row_segments[:, None] == request_ids[None, :], starts[None, :], 0), axis=1
    )


def on_device(
    hidden_in,
    norm_gain,
    query_weight,
    key_weight,
    value_weight,
    out_weight,
    post_gain,
    seg_lengths,
    segment_ids,
    slot_map,
):
    n_group = lax.axis_size("th")
    n_seq = lax.axis_size("seq")
    n_pair = lax.axis_size("tl")
    local_rows = hidden_in.shape[0]
    tokens = segment_ids.shape[0]
    group_rows = local_rows * n_group
    seq_rows = group_rows * n_pair
    head_dim = HD
    half_kv = key_weight.shape[1]
    seq_index = lax.axis_index("seq")
    pair_index = lax.axis_index("tl")
    slot_count = seg_lengths.shape[0]

    hidden = hidden_in.astype(jnp.float32)
    normed = rms_scale(hidden, norm_gain).astype(jnp.bfloat16)

    own_joined = jnp.concatenate([query_weight, key_weight, value_weight], axis=1)
    pair_joined = lax.all_gather(own_joined, "tl", axis=0, tiled=False)
    pair_out = lax.all_gather(out_weight, "tl", axis=0, tiled=True)

    spread = jnp.broadcast_to(normed[None], (n_group,) + normed.shape)
    gathered = lax.all_to_all(spread, "th", 0, 0, tiled=True).reshape(group_rows, -1)
    mixed = jnp.dot(
        gathered,
        jnp.concatenate([pair_joined[0], pair_joined[1]], axis=1),
        preferred_element_type=jnp.float32,
    )
    width = own_joined.shape[1]
    q_first = mixed[:, :head_dim]
    q_second = mixed[:, width : width + head_dim]
    full_key = jnp.concatenate(
        [
            mixed[:, head_dim : head_dim + half_kv],
            mixed[:, width + head_dim : width + head_dim + half_kv],
        ],
        1,
    )
    full_value = jnp.concatenate(
        [mixed[:, head_dim + half_kv : width], mixed[:, width + head_dim + half_kv :]], 1
    )

    member = jnp.arange(group_rows, dtype=jnp.int32) // local_rows
    within = jnp.arange(group_rows, dtype=jnp.int32) % local_rows
    row_ids = seq_index * seq_rows + (member * n_pair + pair_index) * local_rows + within
    row_segments = jnp.take(segment_ids, row_ids)
    positions = row_ids - segment_starts_of(row_segments, seg_lengths)

    q_rot = rotate(jnp.stack([q_first, q_second], axis=1), positions).astype(jnp.bfloat16)
    k_rot = rotate(full_key[:, None, :], positions)[:, 0].astype(jnp.bfloat16)
    v_bf = full_value.astype(jnp.bfloat16)

    kv = jnp.concatenate([k_rot, v_bf], axis=1)
    kv_all = lax.all_gather(kv, ("seq", "tl"), axis=0, tiled=True)
    kv_all = kv_all.reshape(n_seq, n_pair, n_group, local_rows, 2 * head_dim)
    kv_all = jnp.transpose(kv_all, (0, 2, 1, 3, 4)).reshape(tokens, 2 * head_dim)
    key_rows = kv_all[:, :head_dim]
    value_rows = kv_all[:, head_dim:]

    chunk_rows = group_rows // Q_CHUNKS
    member_part = local_rows // Q_CHUNKS
    q_chunks = jnp.transpose(
        q_rot.reshape(n_group, Q_CHUNKS, member_part, 2, head_dim), (1, 0, 2, 3, 4)
    ).reshape(Q_CHUNKS, chunk_rows, 2, head_dim)
    q_ids = jnp.transpose(row_ids.reshape(n_group, Q_CHUNKS, member_part), (1, 0, 2)).reshape(
        Q_CHUNKS, chunk_rows
    )
    q_segs = jnp.transpose(
        row_segments.reshape(n_group, Q_CHUNKS, member_part), (1, 0, 2)
    ).reshape(Q_CHUNKS, chunk_rows)
    q_pos = jnp.transpose(positions.reshape(n_group, Q_CHUNKS, member_part), (1, 0, 2)).reshape(
        Q_CHUNKS, chunk_rows
    )

    def attend(chunk):
        def tile(tile_index, state):
            numer_one, denom_one = state
            k_start = tile_index * KEY_TILE
            k_block = lax.dynamic_slice_in_dim(key_rows, k_start, KEY_TILE, 0)
            v_block = lax.dynamic_slice_in_dim(value_rows, k_start, KEY_TILE, 0)
            k_segs = lax.dynamic_slice_in_dim(segment_ids, k_start, KEY_TILE, 0)
            k_ids = k_start + jnp.arange(KEY_TILE, dtype=jnp.int32)

            scores = (
                jnp.einsum(
                    "qhd,kd->hqk",
                    q_chunks[chunk],
                    k_block,
                    preferred_element_type=jnp.float32,
                )
                * QUERY_SCALE
            )
            scores = SOFTCAP * jnp.tanh(scores / SOFTCAP)
            live = (k_ids[None, :] <= q_ids[chunk][:, None]) & (
                k_segs[None, :] == q_segs[chunk][:, None]
            )
            weights = jnp.where(live[None], jnp.exp(scores - SCORE_SHIFT), 0.0)
            denom_one = denom_one + jnp.sum(weights, axis=-1)
            numer_one = numer_one + jnp.einsum(
                "hqk,kd->qhd",
                weights.astype(jnp.bfloat16),
                v_block,
                preferred_element_type=jnp.float32,
            )
            return (numer_one, denom_one)

        zero_numer = jnp.zeros((chunk_rows, 2, head_dim), jnp.float32)
        zero_denom = jnp.zeros((2, chunk_rows), jnp.float32)
        lo_tile = jnp.min(q_ids[chunk] - q_pos[chunk]) // KEY_TILE
        hi_tile = jnp.max(q_ids[chunk]) // KEY_TILE + 1
        numer, denom = lax.fori_loop(lo_tile, hi_tile, tile, (zero_numer, zero_denom))
        denom_rows = jnp.transpose(denom, (1, 0))[..., None]
        attended = (numer / denom_rows).astype(jnp.bfloat16).reshape(chunk_rows, 2 * head_dim)
        partial = jnp.dot(attended, pair_out, preferred_element_type=jnp.float32).astype(
            jnp.bfloat16
        )
        pieces = lax.all_to_all(
            partial.reshape(n_group, member_part, -1), "th", 0, 0, tiled=True
        )
        return jnp.sum(pieces.astype(jnp.float32), axis=0)

    projected = jnp.concatenate([attend(chunk) for chunk in range(Q_CHUNKS)], axis=0)
    hidden_out = (hidden + rms_scale(projected, post_gain)).astype(jnp.bfloat16)

    cache_len = tokens // 2
    part_len = cache_len // n_seq
    request_ids = jnp.arange(slot_count, dtype=jnp.int32)
    starts = jnp.cumsum(seg_lengths) - seg_lengths
    own_offset = pair_index * half_kv
    own_keys = lax.dynamic_slice_in_dim(key_rows, own_offset, half_kv, 1)
    own_values = lax.dynamic_slice_in_dim(value_rows, own_offset, half_kv, 1)
    keys_pad = jnp.concatenate([own_keys, jnp.zeros((cache_len, half_kv), jnp.bfloat16)], 0)
    values_pad = jnp.concatenate(
        [own_values, jnp.zeros((cache_len, half_kv), jnp.bfloat16)], 0
    )
    seg_pad = jnp.concatenate([segment_ids, jnp.full((cache_len,), -1, jnp.int32)], 0)
    key_slots = []
    value_slots = []
    for slot_index in range(slot_count):
        request = jnp.sum(jnp.where(slot_map == slot_index, request_ids, 0)).astype(jnp.int32)
        first_row = jnp.sum(jnp.where(request_ids == request, starts, 0)).astype(jnp.int32)
        row0 = first_row + seq_index * part_len
        keep = (lax.dynamic_slice_in_dim(seg_pad, row0, part_len, 0) == request)[:, None]
        key_slots.append(
            jnp.where(
                keep,
                lax.dynamic_slice_in_dim(keys_pad, row0, part_len, 0),
                jnp.zeros((), jnp.bfloat16),
            )
        )
        value_slots.append(
            jnp.where(
                keep,
                lax.dynamic_slice_in_dim(values_pad, row0, part_len, 0),
                jnp.zeros((), jnp.bfloat16),
            )
        )
    return (hidden_out, jnp.stack(key_slots), jnp.stack(value_slots))


def solution(mesh):
    devices = np.asarray(mesh.devices)
    n_seq, n_tensor = devices.shape
    split = Mesh(devices.reshape(n_seq, n_tensor // 2, 2), ("seq", "th", "tl"))
    rows = P(("seq", "th", "tl"), None)
    cols = P(None, ("th", "tl"))
    return jax.shard_map(
        on_device,
        mesh=split,
        in_specs=(
            rows,
            P(),
            cols,
            cols,
            cols,
            P(("th", "tl"), None),
            P(),
            P(),
            P(),
            P(),
        ),
        out_specs=(rows, P(None, "seq", ("th", "tl")), P(None, "seq", ("th", "tl"))),
        check_vma=False,
    )
```

profile of v0, /device:TPU:19, one launch (start us, length us, event | category | flops | bytes accessed | tf_op | source)
XLA Modules:
  0.0 451.8 jit_solution(12756819731399506876)
XLA Ops:
  9.7 4.6 %broadcast_in_dim.136 = bf16[16,64,4608]{2,1,0:T(8,128)(2,1)} broadcast(bf16[64,4608]{1,0:T(8,128)(2,1)S(1)} %fusion.26), dimensions={1,2} | broadcast | bytes 10027008 | tf_op jit(solution)/shard_map/broadcast_in_dim | solution.py:79
  14.3 8.6 %all-to-all-start = ((bf16[16,64,4608]{2,1,0:T(8,128)(2,1)}), bf16[16,64,4608]{2,1,0:T(8,128)(2,1)}, u32[]{:S(2)}, u32[]{:S(2)}) async-start(bf16[16,64,4608]{2,1,0:T(8,128)(2,1)} %broadcast_in_dim.136), calls=%async_computation | async-start | bytes 18874368 | tf_op jit(solution)/shard_map/all_to_all | solution.py:80
  24.7 3.5 pad_maximum_fusion
  29.0 6.1 %gather_fusion = s32[1024]{0:T(1024)S(1)} fusion(s32[8192]{0:T(1024)S(1)} %copy-done, s32[1024]{0:T(1024)S(1)} %broadcast_clamp_fusion), kind=kCustom, calls=%fused_computation | custom fusion | bytes 12288 | tf_op jit(solution)/shard_map/jit(_take)/gather | solution.py:103
  36.0 2.6 fusion.64
  38.8 144.7 %all-gather.9.cloned.1.call-done = bf16[9216,256]{1,0:T(8,128)(2,1)} async-done(((bf16[4608,256]{1,0:T(8,128)(2,1)}), bf16[9216,256]{1,0:T(8,128)(2,1)}) %all-gather.9.cloned.1.call-update) | async-done | bytes 4718608 | tf_op jit(solution)/shard_map/all_gather | solution.py:76
  183.5 4.2 fusion.72
  187.6 8.4 %fusion.76 = (bf16[1024,512]{0,1:T(8,128)(2,1)S(1)}, f32[1024,512]{0,1:T(8,128)S(1)}) fusion(bf16[1024,4608]{1,0:T(8,128)(2,1)} %bitcast.18, bf16[4608,256]{1,0:T(8,128)(2,1)} %get-tuple-element.414, bf16[4608,256]{1,0:T(8,128)(2,1)S(1)} %get-tuple-element.413), kind=kOutput, calls=%fused_computation.180 | convolution fusion | flops 4841799680 | bytes 17301504 | tf_op jit(solution)/shard_map/dot_general | solution.py:81
  207.8 28.6 %all-gather.5.cloned.1.call-done = bf16[8192,256]{0,1:T(8,128)(2,1)} async-done(((bf16[1024,256]{0,1:T(8,128)(2,1)}), bf16[8192,256]{0,1:T(8,128)(2,1)}) %all-gather.5.cloned.1.call-update) | async-done | bytes 4194320 | tf_op jit(solution)/shard_map/all_gather | solution.py:111
  236.3 6.4 %copy.51 = bf16[8192,256]{1,0:T(8,128)(2,1)} copy(bf16[8192,256]{0,1:T(8,128)(2,1)} %all-gather.5.cloned.1.call-done) | data formatting | bytes 8388608 | tf_op jit(solution)/shard_map/all_gather | solution.py:111
  242.7 2.5 copy.52
  246.8 2.9 copy.57
  249.8 24.8 %while.29 = (s32[]{:T(128)}, f32[512,2,128]{0,2,1:T(8,128)S(1)}, f32[2,512]{1,0:T(2,128)S(1)}, s32[]{:T(128)}, bf16[8192,128]{0,1:T(8,128)(2,1)}, /*index=5*/s32...) while((s32[]{:T(128)}, f32[512,2,128]{0,2,1:T(8,128)S(1)}, ...), condition=%wide.region_13.14_spmd, body=%wide.region_11.13_spmd.sunk | while | flops 272499200 | bytes 4233419 | solution.py:168
  276.4 5.2 %convolution_convert_fusion = bf16[512,4608]{1,0:T(8,128)(2,1)} fusion(bf16[512,256]{0,1:T(8,128)(2,1)S(1)} %bitcast.128, bf16[256,4608]{1,0:T(8,128)(2,1)} %all-gather.7.cloned.1.call-done), kind=kOutput, calls=%fused_computation.31 | convolution fusion | flops 1210318848 | bytes 7340032 | tf_op jit(solution)/shard_map/dot_general | solution.py:171
  281.6 7.5 %all-to-all-start.2 = ((bf16[16,32,4608]{2,1,0:T(8,128)(2,1)}), bf16[16,32,4608]{2,1,0:T(8,128)(2,1)}, u32[]{:S(2)}, u32[]{:S(2)}) async-start(bf16[16,32,4608]{2,1,0:T(8,128)(2,1)} %bitcast.122), calls=%async_computation.2 | async-start | bytes 9437184 | tf_op jit(solution)/shard_map/all_to_all | solution.py:174
  294.3 24.6 %while.28 = (s32[]{:T(128)}, f32[512,2,128]{0,2,1:T(8,128)S(1)}, f32[2,512]{1,0:T(2,128)S(1)}, s32[]{:T(128)}, bf16[8192,128]{0,1:T(8,128)(2,1)}, /*index=5*/s32...) while((s32[]{:T(128)}, f32[512,2,128]{0,2,1:T(8,128)S(1)}, ...), condition=%wide.region_7.8_spmd, body=%wide.region_5.7_spmd.sunk | while | flops 272499200 | bytes 4233419 | solution.py:168
  319.0 5.3 %convolution_convert_fusion.1 = bf16[512,4608]{1,0:T(8,128)(2,1)} fusion(bf16[512,256]{0,1:T(8,128)(2,1)S(1)} %bitcast.129, bf16[256,4608]{1,0:T(8,128)(2,1)} %all-gather.7.cloned.1.call-done), kind=kOutput, calls=%fused_computation.32 | convolution fusion | flops 1210318848 | bytes 7340032 | tf_op jit(solution)/shard_map/dot_general | solution.py:171
  324.3 37.9 %all-to-all-done.2 = bf16[16,32,4608]{2,1,0:T(8,128)(2,1)} async-done(((bf16[16,32,4608]{2,1,0:T(8,128)(2,1)}), bf16[16,32,4608]{2,1,0:T(8,128)(2,1)}, u32[]{:S(2)}, u32[]{:S(2)}) %all-to-all-start.2) | async-done | bytes 4718624 | tf_op jit(solution)/shard_map/all_to_all | solution.py:174
  362.2 5.2 %all-to-all-start.1 = ((bf16[16,32,4608]{2,1,0:T(8,128)(2,1)}), bf16[16,32,4608]{2,1,0:T(8,128)(2,1)}, u32[]{:S(2)}, u32[]{:S(2)}) async-start(bf16[16,32,4608]{2,1,0:T(8,128)(2,1)} %bitcast.123), calls=%async_computation.1 | async-start | bytes 9437184 | tf_op jit(solution)/shard_map/all_to_all | solution.py:174
  371.3 2.8 constant_dynamic-slice_fusion
  374.0 2.2 select_bitcast_fusion.5
  378.7 3.1 convert_reduce_fusion
  381.8 59.1 %all-to-all-done.1 = bf16[16,32,4608]{2,1,0:T(8,128)(2,1)} async-done(((bf16[16,32,4608]{2,1,0:T(8,128)(2,1)}), bf16[16,32,4608]{2,1,0:T(8,128)(2,1)}, u32[]{:S(2)}, u32[]{:S(2)}) %all-to-all-start.1) | async-done | bytes 4718624 | tf_op jit(solution)/shard_map/all_to_all | solution.py:174
  440.9 3.1 convert_reduce_fusion.1
  (191 shorter events, 70.0 us)
Async XLA Ops:
  14.3 8.7 %copy-start.4 = (bf16[4608,64]{0,1:T(8,128)(2,1)S(1)}, bf16[4608,64]{0,1:T(8,128)(2,1)}, u32[]{:S(2)}) copy-start(bf16[4608,64]{0,1:T(8,128)(2,1)} %param.18) | copy-start | bytes 1769476
  14.3 173.3 %all-to-all-start = ((bf16[16,64,4608]{2,1,0:T(8,128)(2,1)}), bf16[16,64,4608]{2,1,0:T(8,128)(2,1)}, u32[]{:S(2)}, u32[]{:S(2)}) async-start(bf16[16,64,4608]{2,1,0:T(8,128)(2,1)} %broadcast_in_dim.136), calls=%async_computation | async-start | bytes 18874368 | tf_op jit(solution)/shard_map/all_to_all | solution.py:80
  22.9 1.1 copy-start.5
  22.9 160.5 %all-gather.9.cloned.1.call-start = ((), (), s32[]{:S(2)}) async-start(), calls=%async_computation.5 | async-start | bytes 7077888 | tf_op jit(solution)/shard_map/all_gather | solution.py:76
  28.2 0.8 copy-start
  28.2 208.1 %all-gather.5.cloned.1.call-start = ((), (), s32[]{:S(2)}) async-start(), calls=%async_computation.3 | async-start | bytes 4718592 | tf_op jit(solution)/shard_map/all_gather | solution.py:111
  29.0 6.2 %copy-start.7 = (s32[3]{0:T(128)S(1)}, s32[3]{0:T(128)}, u32[]{:S(2)}) copy-start(s32[3]{0:T(128)} %param.21) | copy-start | bytes 40
  29.0 6.4 %copy-start.8 = (s32[3]{0:T(128)S(1)}, s32[3]{0:T(128)}, u32[]{:S(2)}) copy-start(s32[3]{0:T(128)} %param.23) | copy-start | bytes 40
  196.1 1.3 copy-start.2
  197.4 9.1 %copy-start.3 = (f32[1024,512]{0,1:T(8,128)S(1)}, f32[1024,512]{0,1:T(8,128)}, u32[]{:S(2)}) copy-start(f32[1024,512]{0,1:T(8,128)} %copy-done.2) | copy-start | bytes 6291460
  198.3 78.1 %all-gather.7.cloned.1.call-start = ((), (), s32[]{:S(2)}) async-start(), calls=%async_computation.4 | async-start | bytes 3538944 | tf_op jit(solution)/shard_map/all_gather | solution.py:77
  281.6 80.6 %all-to-all-start.2 = ((bf16[16,32,4608]{2,1,0:T(8,128)(2,1)}), bf16[16,32,4608]{2,1,0:T(8,128)(2,1)}, u32[]{:S(2)}, u32[]{:S(2)}) async-start(bf16[16,32,4608]{2,1,0:T(8,128)(2,1)} %bitcast.122), calls=%async_computation.2 | async-start | bytes 9437184 | tf_op jit(solution)/shard_map/all_to_all | solution.py:174
  362.2 78.7 %all-to-all-start.1 = ((bf16[16,32,4608]{2,1,0:T(8,128)(2,1)}), bf16[16,32,4608]{2,1,0:T(8,128)(2,1)}, u32[]{:S(2)}, u32[]{:S(2)}) async-start(bf16[16,32,4608]{2,1,0:T(8,128)(2,1)} %bitcast.123), calls=%async_computation.1 | async-start | bytes 9437184 | tf_op jit(solution)/shard_map/all_to_all | solution.py:174
  381.8 62.5 %copy-start.1 = (bf16[64,4608]{1,0:T(8,128)(2,1)S(1)}, bf16[64,4608]{1,0:T(8,128)(2,1)}, u32[]{:S(2)}) copy-start(bf16[64,4608]{1,0:T(8,128)(2,1)} %param.14) | copy-start | bytes 1769476
  381.8 62.5 %copy-start.6 = (f32[4608]{0:T(1024)S(1)}, f32[4608]{0:T(1024)}, u32[]{:S(2)}) copy-start(f32[4608]{0:T(1024)} %param.20) | copy-start | bytes 55300
Sparse Core Ops, SparseCore 0:
  28.3 155.0 all-gather.8
  198.4 37.8 all-gather.4
  238.0 38.3 all-gather.6
where the time goes:
time: 454 us; the launch traced here: 452 us
  waiting for transfers between devices  273 us (60%)
  matrix products  62 us (14%)
  local copies, waits for them, and re-layouts  38 us (8%)
  other arithmetic  30.4 us (7%)
  between operations  26.2 us (6%)
  starting transfers between devices  21.4 us (5%)
    all_gather x1, waiting for transfers between devices, on_device(): pair_joined = lax.all_gather(own_joined, 'tl', axis=0, tiled=False)  145 us
    all_to_all x2, waiting for transfers between devices, attend(): lax.all_to_all(partial.reshape(n_group, member_part, -1), 'th', 0, 0, til...  97.1 us
    all_gather x1, waiting for transfers between devices, on_device(): kv_all = lax.all_gather(kv, ('seq', 'tl'), axis=0, tiled=True)  28.6 us
    dot_general x14, matrix products, tile(): jnp.einsum('qhd,kd->hqk', q_chunks[chunk], k_block, preferred_element_typ...  25.8 us
    dot_general x14, matrix products, tile(): jnp.einsum('hqk,kd->qhd', weights.astype(jnp.bfloat16), v_block, preferre...  17.2 us
    all_to_all x2, starting transfers between devices, attend(): lax.all_to_all(partial.reshape(n_group, member_part, -1), 'th', 0, 0, til...  12.7 us
    dot_general x2, matrix products, attend(): jnp.dot(attended, pair_out, preferred_element_type=jnp.float32)  10.6 us
  transfers between devices with their start and end apart: 6, of which 5 were waited for; matrix products, arithmetic and copies ran while one was open for 23% of the time, Pallas kernels for 0%

commit v1 on v0

--- a/solution.py
+++ b/solution.py
@@ -77,6 +77,7 @@
     pair_out = lax.all_gather(out_weight, "tl", axis=0, tiled=True)
 
     spread = jnp.broadcast_to(normed[None], (n_group,) + normed.shape)
+    spread, pair_joined = lax.optimization_barrier((spread, pair_joined))
     gathered = lax.all_to_all(spread, "th", 0, 0, tiled=True).reshape(group_rows, -1)
     mixed = jnp.dot(
         gathered,

time: 454 us -> 502 us (1.11)
  the two profiles are of different devices: /device:TPU:19 before, /device:TPU:4 now
where the time goes in v1:
time: 502 us; the launch traced here: 493 us
  waiting for transfers between devices  319 us (64%)
  matrix products  57.3 us (11%)
  local copies, waits for them, and re-layouts  39.7 us (8%)
  other arithmetic  27.6 us (5%)
  between operations  26.5 us (5%)
  starting transfers between devices  22.1 us (4%)
    all_to_all x1, waiting for transfers between devices, on_device(): lax.all_to_all(spread, 'th', 0, 0, tiled=True).reshape(group_rows, -1)  126 us
    all_to_all x2, waiting for transfers between devices, attend(): lax.all_to_all(partial.reshape(n_group, member_part, -1), 'th', 0, 0, til...  92.6 us
    all_gather x1, waiting for transfers between devices, on_device(): pair_joined = lax.all_gather(own_joined, 'tl', axis=0, tiled=False)  66.2 us
    all_gather x1, waiting for transfers between devices, on_device(): kv_all = lax.all_gather(kv, ('seq', 'tl'), axis=0, tiled=True)  27.2 us
    dot_general x12, matrix products, tile(): jnp.einsum('qhd,kd->hqk', q_chunks[chunk], k_block, preferred_element_typ...  23.5 us
    dot_general x12, matrix products, tile(): jnp.einsum('hqk,kd->qhd', weights.astype(jnp.bfloat16), v_block, preferre...  14.8 us
    all_to_all x2, starting transfers between devices, attend(): lax.all_to_all(partial.reshape(n_group, member_part, -1), 'th', 0, 0, til...  14.5 us
    dot_general x2, matrix products, attend(): jnp.dot(attended, pair_out, preferred_element_type=jnp.float32)  10.6 us
  transfers between devices with their start and end apart: 6, of which 6 were waited for; matrix products, arithmetic and copies ran while one was open for 19% of the time, Pallas kernels for 0%

profile of v1, /device:TPU:4, one launch (start us, length us, event | category | flops | bytes accessed | tf_op | source)
XLA Modules:
  0.0 492.9 jit_solution(7991261633840873490)
XLA Ops:
  9.7 3.4 pad_maximum_fusion
  14.6 66.2 %all-gather.9.cloned.1.call-done = bf16[9216,256]{1,0:T(8,128)(2,1)} async-done(((bf16[4608,256]{1,0:T(8,128)(2,1)}), bf16[9216,256]{1,0:T(8,128)(2,1)}) %all-gather.9.cloned.1.call-update) | async-done | bytes 4718608 | tf_op jit(solution)/shard_map/all_gather | solution.py:76
  80.8 4.6 broadcast_in_dim.136
  85.4 7.5 %all-to-all-start = ((bf16[16,64,4608]{2,1,0:T(8,128)(2,1)}), bf16[16,64,4608]{2,1,0:T(8,128)(2,1)}, u32[]{:S(2)}, u32[]{:S(2)}) async-start(bf16[16,64,4608]{2,1,0:T(8,128)(2,1)} %broadcast_in_dim.136), calls=%async_computation | async-start | bytes 18874368 | tf_op jit(solution)/shard_map/all_to_all | solution.py:81
  93.0 6.2 %gather_fusion = s32[1024]{0:T(1024)S(1)} fusion(s32[8192]{0:T(1024)S(1)} %copy-done, s32[1024]{0:T(1024)S(1)} %broadcast_clamp_fusion), kind=kCustom, calls=%fused_computation | custom fusion | bytes 12288 | tf_op jit(solution)/shard_map/jit(_take)/gather | solution.py:104
  100.1 2.6 fusion.64
  102.8 4.2 slice_bitcast_fusion.1
  107.0 125.7 %all-to-all-done = bf16[16,64,4608]{2,1,0:T(8,128)(2,1)} async-done(((bf16[16,64,4608]{2,1,0:T(8,128)(2,1)}), bf16[16,64,4608]{2,1,0:T(8,128)(2,1)}, u32[]{:S(2)}, u32[]{:S(2)}) %all-to-all-start) | async-done | bytes 9437216 | tf_op jit(solution)/shard_map/all_to_all | solution.py:81
  232.6 8.4 %fusion.75 = (bf16[1024,512]{0,1:T(8,128)(2,1)S(1)}, f32[1024,512]{0,1:T(8,128)S(1)}) fusion(bf16[1024,4608]{1,0:T(8,128)(2,1)} %bitcast.19, bf16[4608,256]{1,0:T(8,128)(2,1)} %get-tuple-element.418, bf16[4608,256]{1,0:T(8,128)(2,1)S(1)} %get-tuple-element.417), kind=kOutput, calls=%fused_computation.181 | convolution fusion | flops 4841799680 | bytes 17301504 | tf_op jit(solution)/shard_map/dot_general | solution.py:82
  253.7 27.2 %all-gather.5.cloned.1.call-done = bf16[8192,256]{0,1:T(8,128)(2,1)} async-done(((bf16[1024,256]{0,1:T(8,128)(2,1)}), bf16[8192,256]{0,1:T(8,128)(2,1)}) %all-gather.5.cloned.1.call-update) | async-done | bytes 4194320 | tf_op jit(solution)/shard_map/all_gather | solution.py:112
  280.9 6.4 %copy.51 = bf16[8192,256]{1,0:T(8,128)(2,1)} copy(bf16[8192,256]{0,1:T(8,128)(2,1)} %all-gather.5.cloned.1.call-done) | data formatting | bytes 8388608 | tf_op jit(solution)/shard_map/all_gather | solution.py:112
  291.4 2.9 copy.57
  294.4 21.9 %while.28 = (s32[]{:T(128)}, f32[512,2,128]{0,2,1:T(8,128)S(1)}, f32[2,512]{1,0:T(2,128)S(1)}, s32[]{:T(128)}, bf16[8192,128]{0,1:T(8,128)(2,1)}, /*index=5*/s32...) while((s32[]{:T(128)}, f32[512,2,128]{0,2,1:T(8,128)S(1)}, ...), condition=%wide.region_7.8_spmd, body=%wide.region_5.7_spmd.sunk | while | flops 272499200 | bytes 4233411 | solution.py:169
  316.4 6.5 %all-gather.7.cloned.1.call-done = bf16[256,4608]{1,0:T(8,128)(2,1)} async-done(((bf16[128,4608]{1,0:T(8,128)(2,1)}), bf16[256,4608]{1,0:T(8,128)(2,1)}) %all-gather.7.cloned.1.call-update) | async-done | bytes 2359312 | tf_op jit(solution)/shard_map/all_gather | solution.py:77
  322.9 5.2 %convolution_convert_fusion.1 = bf16[512,4608]{1,0:T(8,128)(2,1)} fusion(bf16[512,256]{0,1:T(8,128)(2,1)S(1)} %bitcast.134, bf16[256,4608]{1,0:T(8,128)(2,1)} %all-gather.7.cloned.1.call-done), kind=kOutput, calls=%fused_computation.32 | convolution fusion | flops 1210318848 | bytes 7340032 | tf_op jit(solution)/shard_map/dot_general | solution.py:172
  328.2 7.3 %all-to-all-start.1 = ((bf16[16,32,4608]{2,1,0:T(8,128)(2,1)}), bf16[16,32,4608]{2,1,0:T(8,128)(2,1)}, u32[]{:S(2)}, u32[]{:S(2)}) async-start(bf16[16,32,4608]{2,1,0:T(8,128)(2,1)} %bitcast.127), calls=%async_computation.1 | async-start | bytes 9437184 | tf_op jit(solution)/shard_map/all_to_all | solution.py:175
  340.8 21.7 %while.29 = (s32[]{:T(128)}, f32[512,2,128]{0,2,1:T(8,128)S(1)}, f32[2,512]{1,0:T(2,128)S(1)}, s32[]{:T(128)}, bf16[8192,128]{0,1:T(8,128)(2,1)}, /*index=5*/s32...) while((s32[]{:T(128)}, f32[512,2,128]{0,2,1:T(8,128)S(1)}, ...), condition=%wide.region_13.14_spmd, body=%wide.region_11.13_spmd.sunk | while | flops 272499200 | bytes 4233411 | solution.py:169
  362.6 5.3 %convolution_convert_fusion = bf16[512,4608]{1,0:T(8,128)(2,1)} fusion(bf16[512,256]{0,1:T(8,128)(2,1)S(1)} %bitcast.135, bf16[256,4608]{1,0:T(8,128)(2,1)} %all-gather.7.cloned.1.call-done), kind=kOutput, calls=%fused_computation.31 | convolution fusion | flops 1210318848 | bytes 7340032 | tf_op jit(solution)/shard_map/dot_general | solution.py:172
  368.0 36.3 %all-to-all-done.1 = bf16[16,32,4608]{2,1,0:T(8,128)(2,1)} async-done(((bf16[16,32,4608]{2,1,0:T(8,128)(2,1)}), bf16[16,32,4608]{2,1,0:T(8,128)(2,1)}, u32[]{:S(2)}, u32[]{:S(2)}) %all-to-all-start.1) | async-done | bytes 4718624 | tf_op jit(solution)/shard_map/all_to_all | solution.py:175
  404.3 7.1 %all-to-all-start.2 = ((bf16[16,32,4608]{2,1,0:T(8,128)(2,1)}), bf16[16,32,4608]{2,1,0:T(8,128)(2,1)}, u32[]{:S(2)}, u32[]{:S(2)}) async-start(bf16[16,32,4608]{2,1,0:T(8,128)(2,1)} %bitcast.128), calls=%async_computation.2 | async-start | bytes 9437184 | tf_op jit(solution)/shard_map/all_to_all | solution.py:175
  415.3 2.8 constant_dynamic-slice_fusion
  422.7 3.1 convert_reduce_fusion.1
  425.8 56.3 %all-to-all-done.2 = bf16[16,32,4608]{2,1,0:T(8,128)(2,1)} async-done(((bf16[16,32,4608]{2,1,0:T(8,128)(2,1)}), bf16[16,32,4608]{2,1,0:T(8,128)(2,1)}, u32[]{:S(2)}, u32[]{:S(2)}) %all-to-all-start.2) | async-done | bytes 4718624 | tf_op jit(solution)/shard_map/all_to_all | solution.py:175
  482.0 3.1 convert_reduce_fusion
  (175 shorter events, 67.3 us)
Async XLA Ops:
  7.2 1.8 copy-start.4
  7.2 73.6 %all-gather.9.cloned.1.call-start = ((), (), s32[]{:S(2)}) async-start(), calls=%async_computation.5 | async-start | bytes 7077888 | tf_op jit(solution)/shard_map/all_gather | solution.py:76
  13.1 1.1 copy-start.1
  13.1 1.3 copy-start.5
  85.4 7.6 %copy-start = (s32[8192]{0:T(1024)S(1)}, s32[8192]{0:T(1024)}, u32[]{:S(2)}) copy-start(s32[8192]{0:T(1024)} %param.22) | copy-start | bytes 98308
  85.4 147.3 %all-to-all-start = ((bf16[16,64,4608]{2,1,0:T(8,128)(2,1)}), bf16[16,64,4608]{2,1,0:T(8,128)(2,1)}, u32[]{:S(2)}, u32[]{:S(2)}) async-start(bf16[16,64,4608]{2,1,0:T(8,128)(2,1)} %broadcast_in_dim.136), calls=%async_computation | async-start | bytes 18874368 | tf_op jit(solution)/shard_map/all_to_all | solution.py:81
  92.9 188.1 %all-gather.5.cloned.1.call-start = ((), (), s32[]{:S(2)}) async-start(), calls=%async_computation.3 | async-start | bytes 4718592 | tf_op jit(solution)/shard_map/all_gather | solution.py:112
  93.0 6.2 %copy-start.7 = (s32[3]{0:T(128)S(1)}, s32[3]{0:T(128)}, u32[]{:S(2)}) copy-start(s32[3]{0:T(128)} %param.21) | copy-start | bytes 40
  93.0 6.4 %copy-start.8 = (s32[3]{0:T(128)S(1)}, s32[3]{0:T(128)}, u32[]{:S(2)}) copy-start(s32[3]{0:T(128)} %param.23) | copy-start | bytes 40
  241.1 1.3 copy-start.2
  242.4 9.3 %copy-start.3 = (f32[1024,512]{0,1:T(8,128)S(1)}, f32[1024,512]{0,1:T(8,128)}, u32[]{:S(2)}) copy-start(f32[1024,512]{0,1:T(8,128)} %copy-done.2) | copy-start | bytes 6291460
  243.3 79.6 %all-gather.7.cloned.1.call-start = ((), (), s32[]{:S(2)}) async-start(), calls=%async_computation.4 | async-start | bytes 3538944 | tf_op jit(solution)/shard_map/all_gather | solution.py:77
  328.2 76.1 %all-to-all-start.1 = ((bf16[16,32,4608]{2,1,0:T(8,128)(2,1)}), bf16[16,32,4608]{2,1,0:T(8,128)(2,1)}, u32[]{:S(2)}, u32[]{:S(2)}) async-start(bf16[16,32,4608]{2,1,0:T(8,128)(2,1)} %bitcast.127), calls=%async_computation.1 | async-start | bytes 9437184 | tf_op jit(solution)/shard_map/all_to_all | solution.py:175
  404.3 77.8 %all-to-all-start.2 = ((bf16[16,32,4608]{2,1,0:T(8,128)(2,1)}), bf16[16,32,4608]{2,1,0:T(8,128)(2,1)}, u32[]{:S(2)}, u32[]{:S(2)}) async-start(bf16[16,32,4608]{2,1,0:T(8,128)(2,1)} %bitcast.128), calls=%async_computation.2 | async-start | bytes 9437184 | tf_op jit(solution)/shard_map/all_to_all | solution.py:175
  425.8 59.6 %copy-start.6 = (f32[4608]{0:T(1024)S(1)}, f32[4608]{0:T(1024)}, u32[]{:S(2)}) copy-start(f32[4608]{0:T(1024)} %param.20) | copy-start | bytes 55300
Sparse Core Ops, SparseCore 0:
  13.2 67.5 all-gather.8
  243.4 37.4 all-gather.4
  282.6 40.2 all-gather.6

commit v2 on v0

--- a/solution.py
+++ b/solution.py
@@ -15,6 +15,7 @@
 ROPE_BASE = 10000.0
 KEY_TILE = 512
 Q_CHUNKS = 2
+HEADS_PER_DEVICE = 4
 
 
 def rms_scale(values, gain):
@@ -59,6 +60,7 @@
     n_group = lax.axis_size("th")
     n_seq = lax.axis_size("seq")
     n_pair = lax.axis_size("tl")
+    kv_local = n_pair // 2
     local_rows = hidden_in.shape[0]
     tokens = segment_ids.shape[0]
     group_rows = local_rows * n_group
@@ -78,24 +80,17 @@
 
     spread = jnp.broadcast_to(normed[None], (n_group,) + normed.shape)
     gathered = lax.all_to_all(spread, "th", 0, 0, tiled=True).reshape(group_rows, -1)
+    width = own_joined.shape[1]
     mixed = jnp.dot(
         gathered,
-        jnp.concatenate([pair_joined[0], pair_joined[1]], axis=1),
+        jnp.concatenate([pair_joined[c] for c in range(n_pair)], axis=1),
         preferred_element_type=jnp.float32,
-    )
-    width = own_joined.shape[1]
-    q_first = mixed[:, :head_dim]
-    q_second = mixed[:, width : width + head_dim]
-    full_key = jnp.concatenate(
-        [
-            mixed[:, head_dim : head_dim + half_kv],
-            mixed[:, width + head_dim : width + head_dim + half_kv],
-        ],
-        1,
-    )
-    full_value = jnp.concatenate(
-        [mixed[:, head_dim + half_kv : width], mixed[:, width + head_dim + half_kv :]], 1
-    )
+    ).reshape(group_rows, n_pair, width)
+    queries = mixed[:, :, :head_dim]
+    full_key = mixed[:, :, head_dim : head_dim + half_kv].reshape(
+        group_rows, kv_local, 2 * half_kv
+    )
+    full_value = mixed[:, :, head_dim + half_kv :].reshape(group_rows, kv_local, 2 * half_kv)
 
     member = jnp.arange(group_rows, dtype=jnp.int32) // local_rows
     within = jnp.arange(group_rows, dtype=jnp.int32) % local_rows
@@ -103,22 +98,22 @@
     row_segments = jnp.take(segment_ids, row_ids)
     positions = row_ids - segment_starts_of(row_segments, seg_lengths)
 
-    q_rot = rotate(jnp.stack([q_first, q_second], axis=1), positions).astype(jnp.bfloat16)
-    k_rot = rotate(full_key[:, None, :], positions)[:, 0].astype(jnp.bfloat16)
+    q_rot = rotate(queries, positions).astype(jnp.bfloat16)
+    k_rot = rotate(full_key, positions).astype(jnp.bfloat16)
     v_bf = full_value.astype(jnp.bfloat16)
 
-    kv = jnp.concatenate([k_rot, v_bf], axis=1)
+    kv = jnp.concatenate([k_rot, v_bf], axis=2)
     kv_all = lax.all_gather(kv, ("seq", "tl"), axis=0, tiled=True)
-    kv_all = kv_all.reshape(n_seq, n_pair, n_group, local_rows, 2 * head_dim)
-    kv_all = jnp.transpose(kv_all, (0, 2, 1, 3, 4)).reshape(tokens, 2 * head_dim)
-    key_rows = kv_all[:, :head_dim]
-    value_rows = kv_all[:, head_dim:]
+    kv_all = kv_all.reshape(n_seq, n_pair, n_group, local_rows, kv_local, 2 * head_dim)
+    kv_all = jnp.transpose(kv_all, (0, 2, 1, 3, 4, 5)).reshape(tokens, kv_local, 2 * head_dim)
+    key_rows = kv_all[:, :, :head_dim]
+    value_rows = kv_all[:, :, head_dim:]
 
     chunk_rows = group_rows // Q_CHUNKS
     member_part = local_rows // Q_CHUNKS
     q_chunks = jnp.transpose(
-        q_rot.reshape(n_group, Q_CHUNKS, member_part, 2, head_dim), (1, 0, 2, 3, 4)
-    ).reshape(Q_CHUNKS, chunk_rows, 2, head_dim)
+        q_rot.reshape(n_group, Q_CHUNKS, member_part, n_pair, head_dim), (1, 0, 2, 3, 4)
+    ).reshape(Q_CHUNKS, chunk_rows, kv_local, 2, head_dim)
     q_ids = jnp.transpose(row_ids.reshape(n_group, Q_CHUNKS, member_part), (1, 0, 2)).reshape(
         Q_CHUNKS, chunk_rows
     )
@@ -140,7 +135,7 @@
 
             scores = (
                 jnp.einsum(
-                    "qhd,kd->hqk",
+                    "qkgd,tkd->kgqt",
                     q_chunks[chunk],
                     k_block,
                     preferred_element_type=jnp.float32,
@@ -151,23 +146,25 @@
             live = (k_ids[None, :] <= q_ids[chunk][:, None]) & (
                 k_segs[None, :] == q_segs[chunk][:, None]
             )
-            weights = jnp.where(live[None], jnp.exp(scores - SCORE_SHIFT), 0.0)
+            weights = jnp.where(live[None, None], jnp.exp(scores - SCORE_SHIFT), 0.0)
             denom_one = denom_one + jnp.sum(weights, axis=-1)
             numer_one = numer_one + jnp.einsum(
-                "hqk,kd->qhd",
+                "kgqt,tkd->qkgd",
                 weights.astype(jnp.bfloat16),
                 v_block,
                 preferred_element_type=jnp.float32,
             )
             return (numer_one, denom_one)
 
-        zero_numer = jnp.zeros((chunk_rows, 2, head_dim), jnp.float32)
-        zero_denom = jnp.zeros((2, chunk_rows), jnp.float32)
+        zero_numer = jnp.zeros((chunk_rows, kv_local, 2, head_dim), jnp.float32)
+        zero_denom = jnp.zeros((kv_local, 2, chunk_rows), jnp.float32)
         lo_tile = jnp.min(q_ids[chunk] - q_pos[chunk]) // KEY_TILE
         hi_tile = jnp.max(q_ids[chunk]) // KEY_TILE + 1
         numer, denom = lax.fori_loop(lo_tile, hi_tile, tile, (zero_numer, zero_denom))
-        denom_rows = jnp.transpose(denom, (1, 0))[..., None]
-        attended = (numer / denom_rows).astype(jnp.bfloat16).reshape(chunk_rows, 2 * head_dim)
+        denom_rows = jnp.transpose(denom, (2, 0, 1))[..., None]
+        attended = (numer / denom_rows).astype(jnp.bfloat16).reshape(
+            chunk_rows, n_pair * head_dim
+        )
         partial = jnp.dot(attended, pair_out, preferred_element_type=jnp.float32).astype(
             jnp.bfloat16
         )
@@ -184,8 +181,10 @@
     request_ids = jnp.arange(slot_count, dtype=jnp.int32)
     starts = jnp.cumsum(seg_lengths) - seg_lengths
     own_offset = pair_index * half_kv
-    own_keys = lax.dynamic_slice_in_dim(key_rows, own_offset, half_kv, 1)
-    own_values = lax.dynamic_slice_in_dim(value_rows, own_offset, half_kv, 1)
+    own_keys = lax.dynamic_slice_in_dim(key_rows.reshape(tokens, -1), own_offset, half_kv, 1)
+    own_values = lax.dynamic_slice_in_dim(
+        value_rows.reshape(tokens, -1), own_offset, half_kv, 1
+    )
     keys_pad = jnp.concatenate([own_keys, jnp.zeros((cache_len, half_kv), jnp.bfloat16)], 0)
     values_pad = jnp.concatenate(
         [own_values, jnp.zeros((cache_len, half_kv), jnp.bfloat16)], 0
@@ -218,7 +217,10 @@
 def solution(mesh):
     devices = np.asarray(mesh.devices)
     n_seq, n_tensor = devices.shape
-    split = Mesh(devices.reshape(n_seq, n_tensor // 2, 2), ("seq", "th", "tl"))
+    split = Mesh(
+        devices.reshape(n_seq, n_tensor // HEADS_PER_DEVICE, HEADS_PER_DEVICE),
+        ("seq", "th", "tl"),
+    )
     rows = P(("seq", "th", "tl"), None)
     cols = P(None, ("th", "tl"))
     return jax.shard_map(

time: 454 us -> 364 us (0.80)
  the two profiles are of different devices: /device:TPU:19 before, /device:TPU:4 now
where the time goes in v2:
time: 364 us; the launch traced here: 369 us
  waiting for transfers between devices  140 us (38%)
  matrix products  94.8 us (26%)
  local copies, waits for them, and re-layouts  60.3 us (17%)
  other arithmetic  29.1 us (8%)
  between operations  25.7 us (7%)
  starting transfers between devices  17.3 us (5%)
    all_gather x1, waiting for transfers between devices, on_device(): pair_joined = lax.all_gather(own_joined, 'tl', axis=0, tiled=False)  77.4 us
    all_gather x1, waiting for transfers between devices, on_device(): kv_all = lax.all_gather(kv, ('seq', 'tl'), axis=0, tiled=True)  58.9 us
    dot_general x24, matrix products, tile(): jnp.einsum('qkgd,tkd->kgqt', q_chunks[chunk], k_block, preferred_element_...  44.6 us
    dot_general x24, matrix products, tile(): jnp.einsum('kgqt,tkd->qkgd', weights.astype(jnp.bfloat16), v_block, prefe...  30.7 us
    slice x2, local copies, waits for them, and re-layouts, on_device(): key_rows = kv_all[:, :, :head_dim]  13.2 us
    dot_general x1, local copies, waits for them, and re-layouts, on_device(): jnp.dot(gathered, jnp.concatenate([pair_joined[c] for c in range(n_pair)]...  12.7 us
    all_to_all x2, starting transfers between devices, attend(): lax.all_to_all(partial.reshape(n_group, member_part, -1), 'th', 0, 0, til...  11.9 us
    dot_general x2, matrix products, attend(): jnp.dot(attended, pair_out, preferred_element_type=jnp.float32)  10.5 us
  transfers between devices with their start and end apart: 6, of which 3 were waited for; matrix products, arithmetic and copies ran while one was open for 42% of the time, Pallas kernels for 0%

profile of v2, /device:TPU:4, one launch (start us, length us, event | category | flops | bytes accessed | tf_op | source)
XLA Modules:
  0.0 369.1 jit_solution(5444898906266470412)
XLA Ops:
  10.5 3.4 pad_maximum_fusion
  15.4 2.6 broadcast_in_dim.133
  18.0 5.2 %all-to-all-start = ((bf16[8,64,4608]{2,1,0:T(8,128)(2,1)}), bf16[8,64,4608]{2,1,0:T(8,128)(2,1)}, u32[]{:S(2)}, u32[]{:S(2)}) async-start(bf16[8,64,4608]{2,1,0:T(8,128)(2,1)} %broadcast_in_dim.133), calls=%async_computation | async-start | bytes 9437184 | tf_op jit(solution)/shard_map/all_to_all | solution.py:82
  23.4 3.1 gather_fusion
  27.5 2.7 fusion.51
  31.1 77.4 %all-gather.9.cloned.1.call-done = bf16[18432,256]{1,0:T(8,128)(2,1)} async-done(((bf16[4608,256]{1,0:T(8,128)(2,1)}), bf16[18432,256]{1,0:T(8,128)(2,1)}) %all-gather.9.cloned.1.call-update) | async-done | bytes 9437200 | tf_op jit(solution)/shard_map/all_gather | solution.py:78
  108.4 4.0 %fusion.58 = (bf16[4608,256]{1,0:T(8,128)(2,1)S(1)}, bf16[4608,256]{1,0:T(8,128)(2,1)S(1)}, bf16[4608,256]{1,0:T(8,128)(2,1)S(1)}, bf16[4608,256]{1,0:T(8,128)(2,1)S(1)}) fusion(bf16[18432,256]{1,0:T(8,128)(2,1)} %all-gather.9.cloned.1.call-done), kind=kLoop, calls=%fused_computation.157 | loop fusion | bytes 18874368 | tf_op jit(solution)/shard_map/slice | solution.py:86
  112.5 4.6 %maximum_bitcast_fusion = bf16[1024,4608]{0,1:T(8,128)(2,1)} fusion(bf16[4608,256]{1,0:T(8,128)(2,1)S(1)} %get-tuple-element.427, bf16[4608,256]{1,0:T(8,128)(2,1)S(1)} %get-tuple-element.425, bf16[4608,256]{1,0:T(8,128)(2,1)S(1)} %get-tuple-element.426, bf16[4608,256]{1,0:T(8,128)(2,1)S(1)} %get-tuple-element.424), kind=kLoop, calls=%fused_computation.29 | loop fusion | flops 37748736 | bytes 18874368 | tf_op jit(solution)/shard_map/dot_general | solution.py:84
  117.1 12.7 %copy.80 = bf16[1024,4608]{1,0:T(8,128)(2,1)} copy(bf16[1024,4608]{0,1:T(8,128)(2,1)} %maximum_bitcast_fusion) | data formatting | bytes 18874368 | tf_op jit(solution)/shard_map/dot_general | solution.py:84
  129.8 9.1 %fusion.61 = f32[512,4,256]{0,2,1:T(8,128)S(1)} fusion(bf16[512,4608,1]{1,0,2:T(8,128)(2,1)} %bitcast.23, bf16[4,256,4608]{2,1,0:T(8,128)(2,1)} %bitcast.134), kind=kOutput, calls=%fused_computation.160 | convolution fusion | flops 4831838208 | bytes 16252928 | tf_op jit(solution)/shard_map/dot_general | solution.py:84
  153.6 58.9 %all-gather.5.cloned.1.call-done = bf16[8192,2,256]{2,0,1:T(8,128)(2,1)} async-done(((bf16[512,2,256]{2,0,1:T(8,128)(2,1)}), bf16[8192,2,256]{2,0,1:T(8,128)(2,1)}) %all-gather.5.cloned.1.call-update) | async-done | bytes 8388624 | tf_op jit(solution)/shard_map/all_gather | solution.py:106
  212.4 8.3 %copy.86 = bf16[4,8,4,64,2,256]{5,3,2,1,0,4:T(8,128)(2,1)} copy(bf16[4,8,4,64,2,256]{5,3,1,2,0,4:T(8,128)(2,1)} %bitcast.137) | data formatting | bytes 16777216 | tf_op jit(solution)/shard_map/transpose | solution.py:108
  220.7 6.9 %fusion.59 = (bf16[8192,2,128]{2,0,1:T(8,128)(2,1)}, bf16[8192,2,128]{2,0,1:T(8,128)(2,1)}) fusion(bf16[8192,2,256]{2,0,1:T(8,128)(2,1)} %bitcast.132), kind=kLoop, calls=%fused_computation.158 | loop fusion | bytes 16777216 | tf_op jit(solution)/shard_map/slice | solution.py:109
  227.6 6.4 %copy.91 = bf16[8192,2,128]{0,2,1:T(8,128)(2,1)} copy(bf16[8192,2,128]{2,0,1:T(8,128)(2,1)} %get-tuple-element.429) | data formatting | bytes 8388608 | tf_op jit(solution)/shard_map/while | solution.py:163
  234.0 41.6 %while.28 = (s32[]{:T(128)}, f32[256,2,2,128]{0,3,2,1:T(8,128)S(1)}, f32[2,2,256]{2,1,0:T(2,128)S(1)}, s32[]{:T(128)}, bf16[8192,2,128]{0,2,1:T(8,128)(2,1)}, /*...) while((s32[]{:T(128)}, ...), condition=%wide.region_7.8_spmd, body=%wide.region_5.7_spmd.sunk | while | flops 272105984 | bytes 4227267 | solution.py:163
  275.6 5.3 %convolution_convert_fusion.1 = bf16[256,4608]{1,0:T(8,128)(2,1)} fusion(bf16[256,512]{0,1:T(8,128)(2,1)S(1)} %bitcast.142, bf16[512,4608]{1,0:T(8,128)(2,1)} %all-gather.7.cloned.1.call-done), kind=kOutput, calls=%fused_computation.31 | convolution fusion | flops 1209139200 | bytes 7340032 | tf_op jit(solution)/shard_map/dot_general | solution.py:168
  281.0 6.2 %all-to-all-start.1 = ((bf16[8,32,4608]{2,1,0:T(8,128)(2,1)}), bf16[8,32,4608]{2,1,0:T(8,128)(2,1)S(1)}, u32[]{:S(2)}, u32[]{:S(2)}) async-start(bf16[8,32,4608]{2,1,0:T(8,128)(2,1)} %bitcast.136), calls=%async_computation.1 | async-start | bytes 4718592 | tf_op jit(solution)/shard_map/all_to_all | solution.py:171
  287.3 42.4 %while.29 = (s32[]{:T(128)}, f32[256,2,2,128]{0,3,2,1:T(8,128)S(1)}, f32[2,2,256]{2,1,0:T(2,128)S(1)}, s32[]{:T(128)}, bf16[8192,2,128]{0,2,1:T(8,128)(2,1)}, /*...) while((s32[]{:T(128)}, ...), condition=%wide.region_13.14_spmd, body=%wide.region_11.13_spmd.sunk | while | flops 272105984 | bytes 4227267 | solution.py:163
  329.7 5.2 %convolution_convert_fusion = bf16[256,4608]{1,0:T(8,128)(2,1)} fusion(bf16[256,512]{0,1:T(8,128)(2,1)S(1)} %bitcast.143, bf16[512,4608]{1,0:T(8,128)(2,1)} %all-gather.7.cloned.1.call-done), kind=kOutput, calls=%fused_computation.30 | convolution fusion | flops 1209139200 | bytes 7340032 | tf_op jit(solution)/shard_map/dot_general | solution.py:168
  334.9 5.7 %all-to-all-start.2 = ((bf16[8,32,4608]{2,1,0:T(8,128)(2,1)}), bf16[8,32,4608]{2,1,0:T(8,128)(2,1)}, u32[]{:S(2)}, u32[]{:S(2)}) async-start(bf16[8,32,4608]{2,1,0:T(8,128)(2,1)} %bitcast.135), calls=%async_computation.2 | async-start | bytes 4718592 | tf_op jit(solution)/shard_map/all_to_all | solution.py:171
  342.4 2.1 fusion.31
  344.5 6.3 %copy.93 = bf16[8192,2,128]{0,2,1:T(8,128)(2,1)} copy(bf16[8192,2,128]{2,0,1:T(8,128)(2,1)} %get-tuple-element.684) | data formatting | bytes 8388608 | tf_op jit(solution)/shard_map/slice | solution.py:109
  355.7 3.5 all-to-all-done.2
  359.2 2.0 convert_reduce_fusion
  (271 shorter events, 100.4 us)
Async XLA Ops:
  7.2 101.2 %all-gather.9.cloned.1.call-start = ((), (), s32[]{:S(2)}) async-start(), calls=%async_computation.5 | async-start | bytes 11796480 | tf_op jit(solution)/shard_map/all_gather | solution.py:78
  13.9 1.1 copy-start.1
  13.9 1.3 copy-start.4
  18.0 5.3 %copy-start = (s32[8192]{0:T(1024)S(1)}, s32[8192]{0:T(1024)}, u32[]{:S(2)}) copy-start(s32[8192]{0:T(1024)} %param.22) | copy-start | bytes 98308
  18.0 8.5 %copy-start.6 = (s32[3]{0:T(128)S(1)}, s32[3]{0:T(128)}, u32[]{:S(2)}) copy-start(s32[3]{0:T(128)} %param.21) | copy-start | bytes 40
  18.0 8.7 %copy-start.7 = (s32[3]{0:T(128)S(1)}, s32[3]{0:T(128)}, u32[]{:S(2)}) copy-start(s32[3]{0:T(128)} %param.23) | copy-start | bytes 40
  18.0 111.7 %all-to-all-start = ((bf16[8,64,4608]{2,1,0:T(8,128)(2,1)}), bf16[8,64,4608]{2,1,0:T(8,128)(2,1)}, u32[]{:S(2)}, u32[]{:S(2)}) async-start(bf16[8,64,4608]{2,1,0:T(8,128)(2,1)} %broadcast_in_dim.133), calls=%async_computation | async-start | bytes 9437184 | tf_op jit(solution)/shard_map/all_to_all | solution.py:82
  23.3 189.2 %all-gather.5.cloned.1.call-start = ((), (), s32[]{:S(2)}) async-start(), calls=%async_computation.3 | async-start | bytes 8912896 | tf_op jit(solution)/shard_map/all_gather | solution.py:106
  140.9 134.7 %all-gather.7.cloned.1.call-start = ((), (), s32[]{:S(2)}) async-start(), calls=%async_computation.4 | async-start | bytes 5898240 | tf_op jit(solution)/shard_map/all_gather | solution.py:79
  275.6 5.4 %copy-start.3 = (bf16[2,256,2,2,128]{4,1,3,2,0:T(8,128)(2,1)}, bf16[2,256,2,2,128]{4,1,3,2,0:T(8,128)(2,1)S(1)}, u32[]{:S(2)}) copy-start(bf16[2,256,2,2,128]{4,1,3,2,0:T(8,128)(2,1)S(1)} %get-tuple-element.700) | copy-start | bytes 1572868
  281.0 53.9 %all-to-all-start.1 = ((bf16[8,32,4608]{2,1,0:T(8,128)(2,1)}), bf16[8,32,4608]{2,1,0:T(8,128)(2,1)S(1)}, u32[]{:S(2)}, u32[]{:S(2)}) async-start(bf16[8,32,4608]{2,1,0:T(8,128)(2,1)} %bitcast.136), calls=%async_computation.1 | async-start | bytes 4718592 | tf_op jit(solution)/shard_map/all_to_all | solution.py:171
  334.9 24.4 %all-to-all-start.2 = ((bf16[8,32,4608]{2,1,0:T(8,128)(2,1)}), bf16[8,32,4608]{2,1,0:T(8,128)(2,1)}, u32[]{:S(2)}, u32[]{:S(2)}) async-start(bf16[8,32,4608]{2,1,0:T(8,128)(2,1)} %bitcast.135), calls=%async_computation.2 | async-start | bytes 4718592 | tf_op jit(solution)/shard_map/all_to_all | solution.py:171
  355.7 5.6 %copy-start.2 = (f32[32,4608]{1,0:T(8,128)S(1)}, f32[32,4608]{1,0:T(8,128)}, u32[]{:S(2)}) copy-start(f32[32,4608]{1,0:T(8,128)} %convert_reduce_fusion.1) | copy-start | bytes 1769476
  355.7 5.8 %copy-start.5 = (f32[4608]{0:T(1024)S(1)}, f32[4608]{0:T(1024)}, u32[]{:S(2)}) copy-start(f32[4608]{0:T(1024)} %param.20) | copy-start | bytes 55300
Sparse Core Ops, SparseCore 0:
  14.0 94.3 all-gather.8
  141.0 71.3 all-gather.4
  214.1 52.8 all-gather.6

commit v3 on v2

--- a/solution.py
+++ b/solution.py
@@ -81,11 +81,9 @@
     spread = jnp.broadcast_to(normed[None], (n_group,) + normed.shape)
     gathered = lax.all_to_all(spread, "th", 0, 0, tiled=True).reshape(group_rows, -1)
     width = own_joined.shape[1]
-    mixed = jnp.dot(
-        gathered,
-        jnp.concatenate([pair_joined[c] for c in range(n_pair)], axis=1),
-        preferred_element_type=jnp.float32,
-    ).reshape(group_rows, n_pair, width)
+    mixed = jnp.einsum(
+        "rd,cdw->rcw", gathered, pair_joined, preferred_element_type=jnp.float32
+    )
     queries = mixed[:, :, :head_dim]
     full_key = mixed[:, :, head_dim : head_dim + half_kv].reshape(
         group_rows, kv_local, 2 * half_kv
@@ -104,10 +102,10 @@
 
     kv = jnp.concatenate([k_rot, v_bf], axis=2)
     kv_all = lax.all_gather(kv, ("seq", "tl"), axis=0, tiled=True)
-    kv_all = kv_all.reshape(n_seq, n_pair, n_group, local_rows, kv_local, 2 * head_dim)
-    kv_all = jnp.transpose(kv_all, (0, 2, 1, 3, 4, 5)).reshape(tokens, kv_local, 2 * head_dim)
-    key_rows = kv_all[:, :, :head_dim]
-    value_rows = kv_all[:, :, head_dim:]
+    kv_all = kv_all.reshape(n_seq, n_pair, n_group, local_rows, kv_local, 2, head_dim)
+    kv_all = jnp.transpose(kv_all, (5, 4, 0, 2, 1, 3, 6)).reshape(2, kv_local, tokens, head_dim)
+    key_rows = kv_all[0]
+    value_rows = kv_all[1]
 
     chunk_rows = group_rows // Q_CHUNKS
     member_part = local_rows // Q_CHUNKS
@@ -128,14 +126,14 @@
         def tile(tile_index, state):
             numer_one, denom_one = state
             k_start = tile_index * KEY_TILE
-            k_block = lax.dynamic_slice_in_dim(key_rows, k_start, KEY_TILE, 0)
-            v_block = lax.dynamic_slice_in_dim(value_rows, k_start, KEY_TILE, 0)
+            k_block = lax.dynamic_slice_in_dim(key_rows, k_start, KEY_TILE, 1)
+            v_block = lax.dynamic_slice_in_dim(value_rows, k_start, KEY_TILE, 1)
             k_segs = lax.dynamic_slice_in_dim(segment_ids, k_start, KEY_TILE, 0)
             k_ids = k_start + jnp.arange(KEY_TILE, dtype=jnp.int32)
 
             scores = (
                 jnp.einsum(
-                    "qkgd,tkd->kgqt",
+                    "qkgd,ktd->kgqt",
                     q_chunks[chunk],
                     k_block,
                     preferred_element_type=jnp.float32,
@@ -149,7 +147,7 @@
             weights = jnp.where(live[None, None], jnp.exp(scores - SCORE_SHIFT), 0.0)
             denom_one = denom_one + jnp.sum(weights, axis=-1)
             numer_one = numer_one + jnp.einsum(
-                "kgqt,tkd->qkgd",
+                "kgqt,ktd->qkgd",
                 weights.astype(jnp.bfloat16),
                 v_block,
                 preferred_element_type=jnp.float32,
@@ -180,10 +178,13 @@
     part_len = cache_len // n_seq
     request_ids = jnp.arange(slot_count, dtype=jnp.int32)
     starts = jnp.cumsum(seg_lengths) - seg_lengths
-    own_offset = pair_index * half_kv
-    own_keys = lax.dynamic_slice_in_dim(key_rows.reshape(tokens, -1), own_offset, half_kv, 1)
+    own_head = pair_index // 2
+    own_offset = pair_index % 2 * half_kv
+    own_keys = lax.dynamic_slice_in_dim(
+        lax.dynamic_index_in_dim(key_rows, own_head, 0, keepdims=False), own_offset, half_kv, 1
+    )
     own_values = lax.dynamic_slice_in_dim(
-        value_rows.reshape(tokens, -1), own_offset, half_kv, 1
+        lax.dynamic_index_in_dim(value_rows, own_head, 0, keepdims=False), own_offset, half_kv, 1
     )
     keys_pad = jnp.concatenate([own_keys, jnp.zeros((cache_len, half_kv), jnp.bfloat16)], 0)
     values_pad = jnp.concatenate(

time: 364 us -> 365 us (level); the launches traced: 369 us -> 362 us
  local copies, waits for them, and re-layouts: 60.3 us -> 67.8 us
  matrix products: 94.8 us -> 88.5 us
  other arithmetic: 29.1 us -> 25.2 us
    all_to_all x1, waiting for transfers between devices: 0.01 us -> 47.4 us  [on_device(): lax.all_to_all(spread, 'th', 0, 0, tiled=True).reshape(group_rows, -1)]
    all_gather x1, waiting for transfers between devices: 77.4 us -> 30.1 us  [on_device(): pair_joined = lax.all_gather(own_joined, 'tl', axis=0, tiled=False)]
    dot_general x1 -> x0, local copies, waits for them, and re-layouts: 12.7 us -> none  [on_device(): jnp.dot(gathered, jnp.concatenate([pair_joined[c] for c in range(n_pair)]...]
    reshape x0 -> x1, local copies, waits for them, and re-layouts: none -> 12.6 us  [on_device(): kv_all.reshape(n_seq, n_pair, n_group, local_rows, kv_local, 2, head_dim)]
    dynamic_slice x1 -> x3, local copies, waits for them, and re-layouts: 1.68 us -> 10.8 us  [the longest x2 8.06 us: on_device(): lax.dynamic_slice_in_dim(lax.dynamic_index_in_dim(value_rows, own_head, 0...]
    transpose x1 -> x0, local copies, waits for them, and re-layouts: 8.25 us -> none  [on_device(): jnp.transpose(kv_all, (0, 2, 1, 3, 4, 5))]
    slice x3, local copies, waits for them, and re-layouts: 17.2 us -> 25.2 us  [the longest x2 22.1 us: on_device(): key_rows = kv_all[0]]
    dot_general x49 -> x45, matrix products: 84.3 us -> 78 us  [the longest x22 40.9 us: tile(): jnp.einsum('qkgd,ktd->kgqt', q_chunks[chunk], k_block, preferred_element_...]
  transfers between devices with their start and end apart: 6 -> 6, of which waited for: 3 -> 3; matrix products, arithmetic and copies ran while one was open for 42% -> 43% of each run, Pallas kernels for 0% -> 0%
where the time goes in v3:
time: 365 us; the launch traced here: 362 us
  waiting for transfers between devices  137 us (38%)
  matrix products  88.5 us (24%)
  local copies, waits for them, and re-layouts  67.8 us (19%)
  between operations  25.5 us (7%)
  other arithmetic  25.2 us (7%)
  starting transfers between devices  17.2 us (5%)
    all_gather x1, waiting for transfers between devices, on_device(): kv_all = lax.all_gather(kv, ('seq', 'tl'), axis=0, tiled=True)  59 us
    all_to_all x1, waiting for transfers between devices, on_device(): lax.all_to_all(spread, 'th', 0, 0, tiled=True).reshape(group_rows, -1)  47.4 us
    dot_general x22, matrix products, tile(): jnp.einsum('qkgd,ktd->kgqt', q_chunks[chunk], k_block, preferred_element_...  40.9 us
    all_gather x1, waiting for transfers between devices, on_device(): pair_joined = lax.all_gather(own_joined, 'tl', axis=0, tiled=False)  30.1 us
    dot_general x22, matrix products, tile(): jnp.einsum('kgqt,ktd->qkgd', weights.astype(jnp.bfloat16), v_block, prefe...  28.1 us
    slice x2, local copies, waits for them, and re-layouts, on_device(): key_rows = kv_all[0]  22.1 us
    reshape x1, local copies, waits for them, and re-layouts, on_device(): kv_all.reshape(n_seq, n_pair, n_group, local_rows, kv_local, 2, head_dim)  12.6 us
    all_to_all x2, starting transfers between devices, attend(): lax.all_to_all(partial.reshape(n_group, member_part, -1), 'th', 0, 0, til...  11.6 us
  transfers between devices with their start and end apart: 6, of which 3 were waited for; matrix products, arithmetic and copies ran while one was open for 43% of the time, Pallas kernels for 0%

profile of v3, /device:TPU:4, one launch (start us, length us, event | category | flops | bytes accessed | tf_op | source)
XLA Modules:
  0.0 362.4 jit_solution(13958650600813720014)
XLA Ops:
  9.7 3.4 pad_maximum_fusion
  14.6 2.5 broadcast_in_dim.133
  17.1 5.2 %all-to-all-start = ((bf16[8,64,4608]{2,1,0:T(8,128)(2,1)}), bf16[8,64,4608]{2,1,0:T(8,128)(2,1)}, u32[]{:S(2)}, u32[]{:S(2)}) async-start(bf16[8,64,4608]{2,1,0:T(8,128)(2,1)} %broadcast_in_dim.133), calls=%async_computation | async-start | bytes 9437184 | tf_op jit(solution)/shard_map/all_to_all | solution.py:82
  22.4 3.1 gather_fusion
  26.5 2.7 fusion.51
  30.1 47.4 %all-to-all-done = bf16[8,64,4608]{2,1,0:T(8,128)(2,1)} async-done(((bf16[8,64,4608]{2,1,0:T(8,128)(2,1)}), bf16[8,64,4608]{2,1,0:T(8,128)(2,1)}, u32[]{:S(2)}, u32[]{:S(2)}) %all-to-all-start) | async-done | bytes 4718624 | tf_op jit(solution)/shard_map/all_to_all | solution.py:82
  77.5 30.1 %all-gather.9.cloned.1.call-done = bf16[18432,256]{1,0:T(8,128)(2,1)} async-done(((bf16[4608,256]{1,0:T(8,128)(2,1)}), bf16[18432,256]{1,0:T(8,128)(2,1)}) %all-gather.9.cloned.1.call-update) | async-done | bytes 9437200 | tf_op jit(solution)/shard_map/all_gather | solution.py:78
  107.6 9.1 %fusion.60 = f32[512,4,256]{0,2,1:T(8,128)S(1)} fusion(bf16[512,4608,1]{1,0,2:T(8,128)(2,1)} %bitcast.23, bf16[4,4608,256]{2,1,0:T(8,128)(2,1)} %bitcast.154), kind=kOutput, calls=%fused_computation.158 | convolution fusion | flops 4831838208 | bytes 16252928 | tf_op jit(solution)/shard_map/rd,cdw->rcw/dot_general | solution.py:84
  131.3 59.0 %all-gather.5.cloned.1.call-done = bf16[8192,2,256]{2,0,1:T(8,128)(2,1)} async-done(((bf16[512,2,256]{2,0,1:T(8,128)(2,1)}), bf16[8192,2,256]{2,0,1:T(8,128)(2,1)}) %all-gather.5.cloned.1.call-update) | async-done | bytes 8388624 | tf_op jit(solution)/shard_map/all_gather | solution.py:104
  190.3 12.6 %reshape.434 = bf16[4,4,8,64,2,2,128]{6,5,3,2,1,0,4:T(2,128)(2,1)} reshape(bf16[8192,2,256]{2,0,1:T(8,128)(2,1)} %all-gather.5.cloned.1.call-done) | data formatting | bytes 16777216 | tf_op jit(solution)/shard_map/reshape | solution.py:105
  202.9 19.0 %fusion.58 = (bf16[1,2,4,8,4,64,128]{6,0,5,3,4,2,1:T(2,128)(2,1)S(1)}, bf16[1,2,4,8,4,64,128]{6,0,5,3,4,2,1:T(2,128)(2,1)S(1)}) fusion(bf16[2,2,4,8,4,64,128]{6,0,5,3,4,2,1:T(2,128)(2,1)} %bitcast.131), kind=kLoop, calls=%fused_computation.156 | loop fusion | bytes 16777216 | tf_op jit(solution)/shard_map/slice | solution.py:107
  221.9 3.0 copy.86
  225.0 3.1 copy.88
  228.1 6.4 %copy.92 = bf16[2,8192,128]{1,2,0:T(8,128)(2,1)} copy(bf16[2,8192,128]{2,1,0:T(8,128)(2,1)} %bitcast.132) | data formatting | bytes 8388608 | tf_op jit(solution)/shard_map/while | solution.py:161
  234.5 37.9 %while.28 = (s32[]{:T(128)}, f32[256,2,2,128]{0,3,2,1:T(8,128)S(1)}, f32[2,2,256]{2,1,0:T(2,128)S(1)}, s32[]{:T(128)}, bf16[2,8192,128]{1,2,0:T(8,128)(2,1)}, /*...) while((s32[]{:T(128)}, ...), condition=%wide.region_7.8_spmd, body=%wide.region_5.7_spmd.sunk | while | flops 272105984 | bytes 4227267 | solution.py:161
  272.5 5.3 %convolution_convert_fusion.1 = bf16[256,4608]{1,0:T(8,128)(2,1)} fusion(bf16[256,512]{0,1:T(8,128)(2,1)S(1)} %bitcast.142, bf16[512,4608]{1,0:T(8,128)(2,1)} %all-gather.7.cloned.1.call-done), kind=kOutput, calls=%fused_computation.30 | convolution fusion | flops 1209139200 | bytes 7340032 | tf_op jit(solution)/shard_map/dot_general | solution.py:166
  277.8 5.9 %all-to-all-start.1 = ((bf16[8,32,4608]{2,1,0:T(8,128)(2,1)}), bf16[8,32,4608]{2,1,0:T(8,128)(2,1)S(1)}, u32[]{:S(2)}, u32[]{:S(2)}) async-start(bf16[8,32,4608]{2,1,0:T(8,128)(2,1)} %bitcast.136), calls=%async_computation.1 | async-start | bytes 4718592 | tf_op jit(solution)/shard_map/all_to_all | solution.py:169
  283.7 38.8 %while.29 = (s32[]{:T(128)}, f32[256,2,2,128]{0,3,2,1:T(8,128)S(1)}, f32[2,2,256]{2,1,0:T(2,128)S(1)}, s32[]{:T(128)}, bf16[2,8192,128]{1,2,0:T(8,128)(2,1)}, /*...) while((s32[]{:T(128)}, ...), condition=%wide.region_13.14_spmd, body=%wide.region_11.13_spmd.sunk | while | flops 272105984 | bytes 4227267 | solution.py:161
  322.6 5.2 %convolution_convert_fusion = bf16[256,4608]{1,0:T(8,128)(2,1)} fusion(bf16[256,512]{0,1:T(8,128)(2,1)S(1)} %bitcast.143, bf16[512,4608]{1,0:T(8,128)(2,1)} %all-gather.7.cloned.1.call-done), kind=kOutput, calls=%fused_computation.29 | convolution fusion | flops 1209139200 | bytes 7340032 | tf_op jit(solution)/shard_map/dot_general | solution.py:166
  327.9 5.7 %all-to-all-start.2 = ((bf16[8,32,4608]{2,1,0:T(8,128)(2,1)}), bf16[8,32,4608]{2,1,0:T(8,128)(2,1)}, u32[]{:S(2)}, u32[]{:S(2)}) async-start(bf16[8,32,4608]{2,1,0:T(8,128)(2,1)} %bitcast.135), calls=%async_computation.2 | async-start | bytes 4718592 | tf_op jit(solution)/shard_map/all_to_all | solution.py:169
  337.4 5.3 %constant_dynamic-slice_fusion = (bf16[1,8192,64]{2,1,0:T(8,128)(2,1)}, bf16[1,8192,64]{2,1,0:T(8,128)(2,1)}) fusion(bf16[2,8192,128]{2,1,0:T(8,128)(2,1)} %bitcast.133, s32[]{:T(128)S(6)} %select_n.246, s32[]{:T(128)S(6)} %select_n.249, bf16[2,8192,128]{2,1,0:T(8,128)(2,1)} %get-tuple-element.661), kind=kLoop, calls=%fused_computation.133 | loop fusion | bytes 4194312 | tf_op jit(solution)/shard_map/dynamic_slice | solution.py:186
  342.7 2.7 copy.94
  345.4 2.7 copy.95
  352.5 2.1 convert_reduce_fusion
  (257 shorter events, 94.1 us)
Async XLA Ops:
  7.2 1.7 copy-start.3
  7.2 100.4 %all-gather.9.cloned.1.call-start = ((), (), s32[]{:S(2)}) async-start(), calls=%async_computation.5 | async-start | bytes 11796480 | tf_op jit(solution)/shard_map/all_gather | solution.py:78
  13.1 1.1 copy-start.1
  13.1 1.3 copy-start.5
  17.1 5.3 %copy-start = (s32[8192]{0:T(1024)S(1)}, s32[8192]{0:T(1024)}, u32[]{:S(2)}) copy-start(s32[8192]{0:T(1024)} %param.22) | copy-start | bytes 98308
  17.1 60.4 %all-to-all-start = ((bf16[8,64,4608]{2,1,0:T(8,128)(2,1)}), bf16[8,64,4608]{2,1,0:T(8,128)(2,1)}, u32[]{:S(2)}, u32[]{:S(2)}) async-start(bf16[8,64,4608]{2,1,0:T(8,128)(2,1)} %broadcast_in_dim.133), calls=%async_computation | async-start | bytes 9437184 | tf_op jit(solution)/shard_map/all_to_all | solution.py:82
  22.3 3.3 copy-start.7
  22.3 3.5 copy-start.8
  22.3 168.0 %all-gather.5.cloned.1.call-start = ((), (), s32[]{:S(2)}) async-start(), calls=%async_computation.3 | async-start | bytes 8912896 | tf_op jit(solution)/shard_map/all_gather | solution.py:104
  118.8 153.7 %all-gather.7.cloned.1.call-start = ((), (), s32[]{:S(2)}) async-start(), calls=%async_computation.4 | async-start | bytes 5898240 | tf_op jit(solution)/shard_map/all_gather | solution.py:79
  272.4 5.4 %copy-start.4 = (bf16[2,256,2,2,128]{4,1,3,2,0:T(8,128)(2,1)}, bf16[2,256,2,2,128]{4,1,3,2,0:T(8,128)(2,1)S(1)}, u32[]{:S(2)}) copy-start(bf16[2,256,2,2,128]{4,1,3,2,0:T(8,128)(2,1)S(1)} %get-tuple-element.674) | copy-start | bytes 1572868
  277.8 50.1 %all-to-all-start.1 = ((bf16[8,32,4608]{2,1,0:T(8,128)(2,1)}), bf16[8,32,4608]{2,1,0:T(8,128)(2,1)S(1)}, u32[]{:S(2)}, u32[]{:S(2)}) async-start(bf16[8,32,4608]{2,1,0:T(8,128)(2,1)} %bitcast.136), calls=%async_computation.1 | async-start | bytes 4718592 | tf_op jit(solution)/shard_map/all_to_all | solution.py:169
  327.9 24.7 %all-to-all-start.2 = ((bf16[8,32,4608]{2,1,0:T(8,128)(2,1)}), bf16[8,32,4608]{2,1,0:T(8,128)(2,1)}, u32[]{:S(2)}, u32[]{:S(2)}) async-start(bf16[8,32,4608]{2,1,0:T(8,128)(2,1)} %bitcast.135), calls=%async_computation.2 | async-start | bytes 4718592 | tf_op jit(solution)/shard_map/all_to_all | solution.py:169
  352.5 2.1 copy-start.2
  352.5 2.3 copy-start.6
Sparse Core Ops, SparseCore 0:
  13.2 94.3 all-gather.8
  118.9 71.3 all-gather.4
  192.0 52.9 all-gather.6

commit v4 on v3

--- a/solution.py
+++ b/solution.py
@@ -13,7 +13,6 @@
 QUERY_SCALE = 144.0 ** (-0.5)
 SCORE_SHIFT = 20.0
 ROPE_BASE = 10000.0
-KEY_TILE = 512
 Q_CHUNKS = 2
 HEADS_PER_DEVICE = 4
 
@@ -100,12 +99,19 @@
     k_rot = rotate(full_key, positions).astype(jnp.bfloat16)
     v_bf = full_value.astype(jnp.bfloat16)
 
-    kv = jnp.concatenate([k_rot, v_bf], axis=2)
-    kv_all = lax.all_gather(kv, ("seq", "tl"), axis=0, tiled=True)
-    kv_all = kv_all.reshape(n_seq, n_pair, n_group, local_rows, kv_local, 2, head_dim)
-    kv_all = jnp.transpose(kv_all, (5, 4, 0, 2, 1, 3, 6)).reshape(2, kv_local, tokens, head_dim)
+    kv = jnp.stack([jnp.transpose(k_rot, (1, 0, 2)), jnp.transpose(v_bf, (1, 0, 2))])
+    kv_all = lax.all_gather(kv, ("seq", "tl"), axis=2, tiled=True)
     key_rows = kv_all[0]
     value_rows = kv_all[1]
+    gathered_index = jnp.arange(tokens, dtype=jnp.int32)
+    block = gathered_index // group_rows
+    in_block = gathered_index % group_rows
+    perm_ids = (
+        block // n_pair * seq_rows
+        + ((in_block // local_rows) * n_pair + block % n_pair) * local_rows
+        + in_block % local_rows
+    )
+    perm_segs = jnp.take(segment_ids, perm_ids)
 
     chunk_rows = group_rows // Q_CHUNKS
     member_part = local_rows // Q_CHUNKS
@@ -125,11 +131,11 @@
     def attend(chunk):
         def tile(tile_index, state):
             numer_one, denom_one = state
-            k_start = tile_index * KEY_TILE
-            k_block = lax.dynamic_slice_in_dim(key_rows, k_start, KEY_TILE, 1)
-            v_block = lax.dynamic_slice_in_dim(value_rows, k_start, KEY_TILE, 1)
-            k_segs = lax.dynamic_slice_in_dim(segment_ids, k_start, KEY_TILE, 0)
-            k_ids = k_start + jnp.arange(KEY_TILE, dtype=jnp.int32)
+            k_start = tile_index * group_rows
+            k_block = lax.dynamic_slice_in_dim(key_rows, k_start, group_rows, 1)
+            v_block = lax.dynamic_slice_in_dim(value_rows, k_start, group_rows, 1)
+            k_segs = lax.dynamic_slice_in_dim(perm_segs, k_start, group_rows, 0)
+            k_ids = lax.dynamic_slice_in_dim(perm_ids, k_start, group_rows, 0)
 
             scores = (
                 jnp.einsum(
@@ -156,8 +162,8 @@
 
         zero_numer = jnp.zeros((chunk_rows, kv_local, 2, head_dim), jnp.float32)
         zero_denom = jnp.zeros((kv_local, 2, chunk_rows), jnp.float32)
-        lo_tile = jnp.min(q_ids[chunk] - q_pos[chunk]) // KEY_TILE
-        hi_tile = jnp.max(q_ids[chunk]) // KEY_TILE + 1
+        lo_tile = jnp.min(q_ids[chunk] - q_pos[chunk]) // seq_rows * n_pair
+        hi_tile = (seq_index + 1) * n_pair
         numer, denom = lax.fori_loop(lo_tile, hi_tile, tile, (zero_numer, zero_denom))
         denom_rows = jnp.transpose(denom, (2, 0, 1))[..., None]
         attended = (numer / denom_rows).astype(jnp.bfloat16).reshape(
@@ -180,12 +186,16 @@
     starts = jnp.cumsum(seg_lengths) - seg_lengths
     own_head = pair_index // 2
     own_offset = pair_index % 2 * half_kv
-    own_keys = lax.dynamic_slice_in_dim(
-        lax.dynamic_index_in_dim(key_rows, own_head, 0, keepdims=False), own_offset, half_kv, 1
-    )
-    own_values = lax.dynamic_slice_in_dim(
-        lax.dynamic_index_in_dim(value_rows, own_head, 0, keepdims=False), own_offset, half_kv, 1
-    )
+
+    def stream_order(rows):
+        own = lax.dynamic_slice_in_dim(
+            lax.dynamic_index_in_dim(rows, own_head, 0, keepdims=False), own_offset, half_kv, 1
+        )
+        own = own.reshape(n_seq, n_pair, n_group, local_rows, half_kv)
+        return jnp.transpose(own, (0, 2, 1, 3, 4)).reshape(tokens, half_kv)
+
+    own_keys = stream_order(key_rows)
+    own_values = stream_order(value_rows)
     keys_pad = jnp.concatenate([own_keys, jnp.zeros((cache_len, half_kv), jnp.bfloat16)], 0)
     values_pad = jnp.concatenate(
         [own_values, jnp.zeros((cache_len, half_kv), jnp.bfloat16)], 0

time: 365 us -> 369 us (1.011)
  local copies, waits for them, and re-layouts: 67.8 us -> 109 us
  waiting for transfers between devices: 137 us -> 96.1 us
  matrix products: 88.5 us -> 94.8 us
  between operations: 25.5 us -> 21.1 us
    gather x0 -> x1, local copies, waits for them, and re-layouts: none -> 45.5 us  [on_device(): perm_segs = jnp.take(segment_ids, perm_ids)]
    all_gather x1, waiting for transfers between devices: 59 us -> 17.8 us  [on_device(): kv_all = lax.all_gather(kv, ('seq', 'tl'), axis=2, tiled=True)]
    slice x2 -> x0, local copies, waits for them, and re-layouts: 22.1 us -> none  [on_device(): key_rows = kv_all[0]]
    transpose x0 -> x2, local copies, waits for them, and re-layouts: none -> 10.6 us  [stream_order(): return jnp.transpose(own, (0, 2, 1, 3, 4)).reshape(tokens, half_kv)]
    slice x1, local copies, waits for them, and re-layouts: 3.05 us -> 8.71 us  [on_device(): value_rows = kv_all[1]]
    dynamic_slice x25 -> x49, local copies, waits for them, and re-layouts: 12.5 us -> 17.3 us  [the longest x24 10.1 us: tile(): k_segs = lax.dynamic_slice_in_dim(perm_segs, k_start, group_rows, 0)]
    dot_general x22 -> x24, matrix products: 40.9 us -> 44.6 us  [tile(): jnp.einsum('qkgd,ktd->kgqt', q_chunks[chunk], k_block, preferred_element_...]
    reshape x1 -> x2, local copies, waits for them, and re-layouts: 12.6 us -> 9.19 us  [stream_order(): return jnp.transpose(own, (0, 2, 1, 3, 4)).reshape(tokens, half_kv)]
  transfers between devices with their start and end apart: 6 -> 6, of which waited for: 3 -> 3; matrix products, arithmetic and copies ran while one was open for 43% -> 56% of each run, Pallas kernels for 0% -> 0%
where the time goes in v4:
time: 369 us; the launch traced here: 365 us
  local copies, waits for them, and re-layouts  109 us (30%)
  waiting for transfers between devices  96.1 us (26%)
  matrix products  94.8 us (26%)
  other arithmetic  25.5 us (7%)
  between operations  21.1 us (6%)
  starting transfers between devices  17 us (5%)
    all_to_all x1, waiting for transfers between devices, on_device(): lax.all_to_all(spread, 'th', 0, 0, tiled=True).reshape(group_rows, -1)  47.5 us
    gather x1, local copies, waits for them, and re-layouts, on_device(): perm_segs = jnp.take(segment_ids, perm_ids)  45.5 us
    dot_general x24, matrix products, tile(): jnp.einsum('qkgd,ktd->kgqt', q_chunks[chunk], k_block, preferred_element_...  44.6 us
    dot_general x24, matrix products, tile(): jnp.einsum('kgqt,ktd->qkgd', weights.astype(jnp.bfloat16), v_block, prefe...  30.6 us
    all_gather x1, waiting for transfers between devices, on_device(): pair_joined = lax.all_gather(own_joined, 'tl', axis=0, tiled=False)  30.1 us
    all_gather x1, waiting for transfers between devices, on_device(): kv_all = lax.all_gather(kv, ('seq', 'tl'), axis=2, tiled=True)  17.8 us
    all_to_all x2, starting transfers between devices, attend(): lax.all_to_all(partial.reshape(n_group, member_part, -1), 'th', 0, 0, til...  11.7 us
    transpose x2, local copies, waits for them, and re-layouts, stream_order(): return jnp.transpose(own, (0, 2, 1, 3, 4)).reshape(tokens, half_kv)  10.6 us
  transfers between devices with their start and end apart: 6, of which 3 were waited for; matrix products, arithmetic and copies ran while one was open for 56% of the time, Pallas kernels for 0%

profile of v4, /device:TPU:4, one launch (start us, length us, event | category | flops | bytes accessed | tf_op | source)
XLA Modules:
  0.0 364.9 jit_solution(3421114902233199308)
XLA Ops:
  9.7 3.4 pad_maximum_fusion
  14.6 2.5 broadcast_in_dim.139
  17.1 5.2 %all-to-all-start = ((bf16[8,64,4608]{2,1,0:T(8,128)(2,1)}), bf16[8,64,4608]{2,1,0:T(8,128)(2,1)}, u32[]{:S(2)}, u32[]{:S(2)}) async-start(bf16[8,64,4608]{2,1,0:T(8,128)(2,1)} %broadcast_in_dim.139), calls=%async_computation | async-start | bytes 9437184 | tf_op jit(solution)/shard_map/all_to_all | solution.py:81
  22.4 3.1 gather_fusion
  26.5 2.6 fusion.80
  30.0 47.5 %all-to-all-done = bf16[8,64,4608]{2,1,0:T(8,128)(2,1)} async-done(((bf16[8,64,4608]{2,1,0:T(8,128)(2,1)}), bf16[8,64,4608]{2,1,0:T(8,128)(2,1)}, u32[]{:S(2)}, u32[]{:S(2)}) %all-to-all-start) | async-done | bytes 4718624 | tf_op jit(solution)/shard_map/all_to_all | solution.py:81
  77.5 30.1 %all-gather.9.cloned.1.call-done = bf16[18432,256]{1,0:T(8,128)(2,1)} async-done(((bf16[4608,256]{1,0:T(8,128)(2,1)}), bf16[18432,256]{1,0:T(8,128)(2,1)}) %all-gather.9.cloned.1.call-update) | async-done | bytes 9437200 | tf_op jit(solution)/shard_map/all_gather | solution.py:77
  107.6 9.1 %fusion.89 = f32[512,4,256]{0,2,1:T(8,128)S(1)} fusion(bf16[512,4608,1]{1,0,2:T(8,128)(2,1)} %bitcast.23, bf16[4,4608,256]{2,1,0:T(8,128)(2,1)} %bitcast.169), kind=kOutput, calls=%fused_computation.220 | convolution fusion | flops 4831838208 | bytes 16252928 | tf_op jit(solution)/shard_map/rd,cdw->rcw/dot_general | solution.py:83
  125.9 45.5 %gather_fusion.1 = s32[8192]{0:T(1024)S(1)} fusion(s32[8192]{0:T(1024)S(1)} %copy-done, s32[8192]{0:T(1024)S(1)} %broadcast_clamp_fusion), kind=kCustom, calls=%fused_computation.1 | custom fusion | bytes 98304 | tf_op jit(solution)/shard_map/jit(_take)/gather | solution.py:114
  172.5 17.8 %all-gather.5.cloned.1.call-done = bf16[2,2,8192,128]{3,2,1,0:T(8,128)(2,1)} async-done(((bf16[2,2,512,128]{3,2,1,0:T(8,128)(2,1)}), bf16[2,2,8192,128]{3,2,1,0:T(8,128)(2,1)}) %all-gather.5.cloned.1.call-update) | async-done | bytes 8388624 | tf_op jit(solution)/shard_map/all_gather | solution.py:103
  190.3 8.7 %fusion.87 = (bf16[1,2,8192,128]{3,2,1,0:T(8,128)(2,1)}, bf16[2,8192,128]{2,1,0:T(8,128)(2,1)}, bf16[2,8192,128]{2,1,0:T(8,128)(2,1)}, bf16[1,2,8192,128]{3,2,1,0:T(8,128)(2,1)}) fusion(bf16[2,2,8192,128]{3,2,1,0:T(8,128)(2,1)} %all-gather.5.cloned.1.call-done), kind=kLoop, calls=%fused_computation.218 | loop fusion | bytes 25165824 | tf_op jit(solution)/shard_map/slice | solution.py:105
  199.0 6.4 %copy.73 = bf16[2,8192,128]{1,2,0:T(8,128)(2,1)} copy(bf16[2,8192,128]{2,1,0:T(8,128)(2,1)} %get-tuple-element.415) | data formatting | bytes 8388608 | tf_op jit(solution)/shard_map/while | solution.py:167
  205.5 42.4 %while.28 = (s32[]{:T(128)}, f32[256,2,2,128]{0,3,2,1:T(8,128)S(1)}, f32[2,2,256]{2,1,0:T(2,128)S(1)}, s32[]{:T(128)}, bf16[2,8192,128]{1,2,0:T(8,128)(2,1)}, /*...) while((s32[]{:T(128)}, ...), condition=%wide.region_6.7_spmd, body=%wide.region_4.6_spmd.sunk | while | flops 272105472 | bytes 4229323 | solution.py:167
  248.0 5.3 %convolution_convert_fusion.1 = bf16[256,4608]{1,0:T(8,128)(2,1)} fusion(bf16[256,512]{0,1:T(8,128)(2,1)S(1)} %bitcast.155, bf16[512,4608]{1,0:T(8,128)(2,1)} %all-gather.7.cloned.1.call-done), kind=kOutput, calls=%fused_computation.29 | convolution fusion | flops 1209139200 | bytes 7340032 | tf_op jit(solution)/shard_map/dot_general | solution.py:172
  253.3 6.0 %all-to-all-start.1 = ((bf16[8,32,4608]{2,1,0:T(8,128)(2,1)}), bf16[8,32,4608]{2,1,0:T(8,128)(2,1)S(1)}, u32[]{:S(2)}, u32[]{:S(2)}) async-start(bf16[8,32,4608]{2,1,0:T(8,128)(2,1)} %bitcast.149), calls=%async_computation.1 | async-start | bytes 4718592 | tf_op jit(solution)/shard_map/all_to_all | solution.py:175
  259.3 51.4 %while.29 = (s32[]{:T(128)}, f32[256,2,2,128]{0,3,2,1:T(8,128)S(1)}, f32[2,2,256]{2,1,0:T(2,128)S(1)}, s32[]{:T(128)}, bf16[2,8192,128]{1,2,0:T(8,128)(2,1)}, /*...) while((s32[]{:T(128)}, ...), condition=%wide.region_11.12_spmd, body=%wide.region_9.11_spmd.sunk | while | flops 272105472 | bytes 4229323 | solution.py:167
  310.8 5.2 %convolution_convert_fusion = bf16[256,4608]{1,0:T(8,128)(2,1)} fusion(bf16[256,512]{0,1:T(8,128)(2,1)S(1)} %bitcast.156, bf16[512,4608]{1,0:T(8,128)(2,1)} %all-gather.7.cloned.1.call-done), kind=kOutput, calls=%fused_computation.28 | convolution fusion | flops 1209139200 | bytes 7340032 | tf_op jit(solution)/shard_map/dot_general | solution.py:172
  315.9 5.7 %all-to-all-start.2 = ((bf16[8,32,4608]{2,1,0:T(8,128)(2,1)}), bf16[8,32,4608]{2,1,0:T(8,128)(2,1)}, u32[]{:S(2)}, u32[]{:S(2)}) async-start(bf16[8,32,4608]{2,1,0:T(8,128)(2,1)} %bitcast.148), calls=%async_computation.2 | async-start | bytes 4718592 | tf_op jit(solution)/shard_map/all_to_all | solution.py:175
  325.4 5.4 %constant_dynamic-slice_fusion = (bf16[1,1,8192,64]{3,2,1,0:T(8,128)(2,1)}, bf16[1,1,8192,64]{3,2,1,0:T(8,128)(2,1)}) fusion(bf16[1,2,8192,128]{3,2,1,0:T(8,128)(2,1)} %get-tuple-element.414, s32[]{:T(128)S(6)} %select_n.389, s32[]{:T(128)S(6)} %select_n.392, bf16[1,2,8192,128]{3,2,1,0:T(8,128)(2,1)} %get-tuple-element.417), kind=kLoop, calls=%fused_computation.193 | loop fusion | bytes 4194312 | tf_op jit(solution)/shard_map/dynamic_slice | solution.py:191
  330.9 5.3 %copy.76 = bf16[4,8,4,64,64]{3,2,1,0,4:T(4,128)(2,1)} copy(bf16[4,8,4,64,64]{4,3,1,2,0:T(8,128)(2,1)} %bitcast.151) | data formatting | bytes 2097152 | tf_op jit(solution)/shard_map/transpose | solution.py:195
  336.2 4.6 %reshape.652 = bf16[8192,64]{0,1:T(8,128)(2,1)} reshape(bf16[4,8,4,64,64]{3,2,1,0,4:T(4,128)(2,1)} %copy.76) | data formatting | bytes 2097152 | tf_op jit(solution)/shard_map/reshape | solution.py:195
  340.8 5.3 %copy.78 = bf16[4,8,4,64,64]{3,2,1,0,4:T(4,128)(2,1)} copy(bf16[4,8,4,64,64]{4,3,1,2,0:T(8,128)(2,1)} %bitcast.150) | data formatting | bytes 2097152 | tf_op jit(solution)/shard_map/transpose | solution.py:195
  346.0 4.6 %reshape.654 = bf16[8192,64]{0,1:T(8,128)(2,1)} reshape(bf16[4,8,4,64,64]{3,2,1,0,4:T(4,128)(2,1)} %copy.78) | data formatting | bytes 2097152 | tf_op jit(solution)/shard_map/reshape | solution.py:195
  355.0 2.1 convert_reduce_fusion
  (279 shorter events, 111.0 us)
Async XLA Ops:
  7.2 1.7 copy-start.3
  7.2 100.4 %all-gather.9.cloned.1.call-start = ((), (), s32[]{:S(2)}) async-start(), calls=%async_computation.5 | async-start | bytes 11796480 | tf_op jit(solution)/shard_map/all_gather | solution.py:77
  13.1 1.1 copy-start.1
  13.1 1.3 copy-start.6
  17.1 5.3 %copy-start = (s32[8192]{0:T(1024)S(1)}, s32[8192]{0:T(1024)}, u32[]{:S(2)}) copy-start(s32[8192]{0:T(1024)} %param.22) | copy-start | bytes 98308
  17.1 60.4 %all-to-all-start = ((bf16[8,64,4608]{2,1,0:T(8,128)(2,1)}), bf16[8,64,4608]{2,1,0:T(8,128)(2,1)}, u32[]{:S(2)}, u32[]{:S(2)}) async-start(bf16[8,64,4608]{2,1,0:T(8,128)(2,1)} %broadcast_in_dim.139), calls=%async_computation | async-start | bytes 9437184 | tf_op jit(solution)/shard_map/all_to_all | solution.py:81
  22.3 3.3 copy-start.8
  22.3 3.5 copy-start.9
  22.3 167.9 %all-gather.5.cloned.1.call-start = ((), (), s32[]{:S(2)}) async-start(), calls=%async_computation.3 | async-start | bytes 8912896 | tf_op jit(solution)/shard_map/all_gather | solution.py:103
  118.8 129.2 %all-gather.7.cloned.1.call-start = ((), (), s32[]{:S(2)}) async-start(), calls=%async_computation.4 | async-start | bytes 5898240 | tf_op jit(solution)/shard_map/all_gather | solution.py:78
  247.9 5.4 %copy-start.4 = (bf16[2,256,2,2,128]{4,1,3,2,0:T(8,128)(2,1)}, bf16[2,256,2,2,128]{4,1,3,2,0:T(8,128)(2,1)S(1)}, u32[]{:S(2)}) copy-start(bf16[2,256,2,2,128]{4,1,3,2,0:T(8,128)(2,1)S(1)} %get-tuple-element.703) | copy-start | bytes 1572868
  247.9 5.4 %copy-start.5 = (s32[8192]{0:T(1024)}, s32[8192]{0:T(1024)S(1)}, u32[]{:S(2)}) copy-start(s32[8192]{0:T(1024)S(1)} %get-tuple-element.705) | copy-start | bytes 98308
  253.3 62.7 %all-to-all-start.1 = ((bf16[8,32,4608]{2,1,0:T(8,128)(2,1)}), bf16[8,32,4608]{2,1,0:T(8,128)(2,1)S(1)}, u32[]{:S(2)}, u32[]{:S(2)}) async-start(bf16[8,32,4608]{2,1,0:T(8,128)(2,1)} %bitcast.149), calls=%async_computation.1 | async-start | bytes 4718592 | tf_op jit(solution)/shard_map/all_to_all | solution.py:175
  315.9 39.0 %all-to-all-start.2 = ((bf16[8,32,4608]{2,1,0:T(8,128)(2,1)}), bf16[8,32,4608]{2,1,0:T(8,128)(2,1)}, u32[]{:S(2)}, u32[]{:S(2)}) async-start(bf16[8,32,4608]{2,1,0:T(8,128)(2,1)} %bitcast.148), calls=%async_computation.2 | async-start | bytes 4718592 | tf_op jit(solution)/shard_map/all_to_all | solution.py:175
  354.9 2.1 copy-start.2
  354.9 2.3 copy-start.7
Sparse Core Ops, SparseCore 0:
  13.2 94.3 all-gather.8
  118.9 71.3 all-gather.4
  191.9 52.8 all-gather.6
